TPU v7x, 256 devices: a whole 4x4x8 slice. The times are simulated.
256 devices in a mesh: prompt: 16 (over x_hi, z), resp: 8 (over x_lo, y), head: 2 (over core).
Axes of the slice: x: 4 (x_hi: 2, x_lo: 2; x = x_hi * 2 + x_lo), y: 4, z: 8, core: 2. Of those that a mesh axis runs over, the one named last changes fastest.
Arguments:
- prompt_q: bfloat16 [8, 1024, 4, 512], P('resp', 'prompt', None, 'head'), may hold values from -250 to 250
- prompt_kv: bfloat16 [2, 8, 1024, 512], P(None, 'resp', 'prompt'), may hold values from -8 to 8
- prompt_grad: bfloat16 [8, 1024, 4, 512], P('resp', 'prompt', None, 'head'), may hold values from -6 to 6
- resp_q: bfloat16 [16, 8, 8, 64, 4, 512], P('prompt', 'resp', None, None, None, 'head'), may hold values from -250 to 250
- resp_kv: bfloat16 [2, 16, 8, 8, 64, 512], P(None, 'prompt', 'resp'), may hold values from -6 to 6
- resp_grad: bfloat16 [16, 8, 8, 64, 4, 512], P('prompt', 'resp', None, None, None, 'head'), may hold values from -6 to 6
- resp_prompt: int32 [16, 8, 8], P('prompt', 'resp'), may hold values from 0 to 7, as said below
Outputs:
- prompt_out: bfloat16 [8, 1024, 4, 512], P('resp', 'prompt', None, 'head')
- prompt_dq: bfloat16 [8, 1024, 4, 512], P('resp', 'prompt', None, 'head')
- prompt_dkv: bfloat16 [2, 8, 1024, 512], P(None, 'resp', 'prompt', 'head')
- resp_out: bfloat16 [16, 8, 8, 64, 4, 512], P('prompt', 'resp', None, None, None, 'head')
- resp_dq: bfloat16 [16, 8, 8, 64, 4, 512], P('prompt', 'resp', None, None, None, 'head')
- resp_dkv: bfloat16 [2, 16, 8, 8, 64, 512], P(None, 'prompt', 'resp', None, None, 'head')
Inputs may be any that keep to these rules, and one draw needn't show every extreme that they name: `resp_prompt`: entry [p, r, j] is the prompt of response j held at prompt index p and resp index r; each row of 8 entries names every prompt once.
All inputs are finite; a program needn't handle non-finite values.
Results may differ from a plain program's by a relative error of at most 0.0095.
Values may be sent and summed in bfloat16 or wider, within the bound.
No kernel may reach another device: no remote copies, remote signals or barrier semaphores. Data moves between devices by JAX's collectives and lax.ppermute only.
A program may use at most 128 MiB of HBM per device.

v0:
```python
import math

import jax
import jax.numpy as jnp
from jax import lax
from jax.sharding import PartitionSpec as P

HD = 128


def attend(queries, keys_in, values_in, cotangent, allowed):
    scale = 1.0 / math.sqrt(HD)
    scores = (
        jnp.einsum("brkgd,bnkd->bkgrn", queries, keys_in, preferred_element_type=jnp.float32)
        * scale
    )
    scores = jnp.where(allowed, scores, -1e30)
    row_max = jnp.max(scores, axis=-1, keepdims=True)
    totals = jnp.sum(jnp.exp(scores - row_max), axis=-1, keepdims=True)
    log_total = row_max + jnp.log(totals)
    probabilities = jnp.exp(scores - log_total)
    weights = probabilities.astype(jnp.bfloat16)
    output = jnp.einsum(
        "bkgrn,bnkd->brkgd", weights, values_in, preferred_element_type=jnp.float32
    ).astype(jnp.bfloat16)
    row_delta = jnp.einsum(
        "brkgd,brkgd->bkgr", cotangent, output, preferred_element_type=jnp.float32
    )
    dprobs = jnp.einsum(
        "brkgd,bnkd->bkgrn", cotangent, values_in, preferred_element_type=jnp.float32
    )
    dscores = (probabilities * (dprobs - row_delta[..., None])).astype(jnp.bfloat16)
    dquery = (
        jnp.einsum("bkgrn,bnkd->brkgd", dscores, keys_in, preferred_element_type=jnp.float32)
        * scale
    )
    dkeys = (
        jnp.einsum("bkgrn,brkgd->bnkd", dscores, queries, preferred_element_type=jnp.float32)
        * scale
    )
    dvalues = jnp.einsum(
        "bkgrn,brkgd->bnkd", weights, cotangent, preferred_element_type=jnp.float32
    )
    return (output, dquery, dkeys, dvalues)


def body(prompt_q, prompt_kv, prompt_grad, resp_q, resp_kv, resp_grad, resp_prompt):
    head_size = HD
    block_rows = prompt_q.shape[1]
    kv_heads = prompt_q.shape[2]
    local_width = prompt_q.shape[3]
    local_heads = local_width // head_size
    full_len = block_rows * lax.axis_size("prompt")
    resp_len = resp_q.shape[3]
    peers = lax.axis_size("resp")
    kv_width = kv_heads * head_size
    gathered = lax.all_gather(prompt_kv, "prompt", axis=2, tiled=True)
    prompt_keys = gathered[0, 0].reshape(1, full_len, kv_heads, head_size)
    prompt_values = gathered[1, 0].reshape(1, full_len, kv_heads, head_size)
    query_rows = lax.axis_index("prompt") * block_rows + jnp.arange(block_rows)
    key_cols = jnp.arange(full_len)
    causal = key_cols[None, :] <= query_rows[:, None]
    queries = prompt_q.reshape(1, block_rows, kv_heads, local_heads, head_size)
    cotangent = prompt_grad.reshape(1, block_rows, kv_heads, local_heads, head_size)
    p_out, p_dq, p_dk, p_dv = attend(queries, prompt_keys, prompt_values, cotangent, causal)
    order = resp_prompt[0, 0]
    picker = (jnp.arange(peers)[:, None] == order[None, :]).astype(jnp.bfloat16)
    send_q = jnp.einsum(
        "dj,jrkh->drkh", picker, resp_q[0, 0], preferred_element_type=jnp.float32
    ).astype(jnp.bfloat16)
    send_kv = jnp.einsum(
        "dj,cjrh->dcrh", picker, resp_kv[:, 0, 0], preferred_element_type=jnp.float32
    ).astype(jnp.bfloat16)
    send_grad = jnp.einsum(
        "dj,jrkh->drkh", picker, resp_grad[0, 0], preferred_element_type=jnp.float32
    ).astype(jnp.bfloat16)
    got_q, got_kv, got_grad = (
        lax.all_to_all(send_q, "resp", split_axis=0, concat_axis=0, tiled=True),
        lax.all_to_all(send_kv, "resp", split_axis=0, concat_axis=0, tiled=True),
        lax.all_to_all(send_grad, "resp", split_axis=0, concat_axis=0, tiled=True),
    )
    steps_own = jnp.arange(resp_len)
    allowed = jnp.concatenate(
        [jnp.ones((resp_len, full_len), bool), steps_own[None, :] <= steps_own[:, None]], axis=1
    )

    def one_response(carry, item):
        slot_q, slot_kv, slot_grad = item
        keys_all = jnp.concatenate(
            [prompt_keys[0], slot_kv[0].reshape(resp_len, kv_heads, head_size)], axis=0
        )[None]
        values_all = jnp.concatenate(
            [prompt_values[0], slot_kv[1].reshape(resp_len, kv_heads, head_size)], axis=0
        )[None]
        r_out, r_dq, r_dk, r_dv = attend(
            slot_q.reshape(1, resp_len, kv_heads, local_heads, head_size),
            keys_all,
            values_all,
            slot_grad.reshape(1, resp_len, kv_heads, local_heads, head_size),
            allowed,
        )
        carry = carry + jnp.stack([r_dk[0, :full_len], r_dv[0, :full_len]])
        own_grads = jnp.stack([r_dk[0, full_len:], r_dv[0, full_len:]]).reshape(
            2, resp_len, kv_width
        )
        return (
            carry,
            (
                r_out.reshape(resp_len, kv_heads, local_width),
                r_dq.astype(jnp.bfloat16).reshape(resp_len, kv_heads, local_width),
                own_grads,
            ),
        )

    start = jnp.stack([p_dk[0], p_dv[0]])
    summed, (back_out, back_dq, own_part) = lax.scan(one_response, start, (got_q, got_kv, got_grad))
    prompt_part = summed.reshape(2, full_len, kv_width)
    rows_sum = lax.psum_scatter(prompt_part, "prompt", scatter_dimension=1, tiled=True)
    block_sum, own_sum = (
        lax.psum_scatter(rows_sum, "head", scatter_dimension=2, tiled=True),
        lax.psum_scatter(own_part, "head", scatter_dimension=3, tiled=True),
    )
    prompt_dkv = block_sum.astype(jnp.bfloat16)[:, None]
    back_kv = own_sum.astype(jnp.bfloat16)
    ret_out, ret_dq, ret_kv = (
        lax.all_to_all(back_out, "resp", split_axis=0, concat_axis=0, tiled=True),
        lax.all_to_all(back_dq, "resp", split_axis=0, concat_axis=0, tiled=True),
        lax.all_to_all(back_kv, "resp", split_axis=0, concat_axis=0, tiled=True),
    )
    resp_out = jnp.einsum(
        "dj,drkh->jrkh", picker, ret_out, preferred_element_type=jnp.float32
    ).astype(jnp.bfloat16)[None, None]
    resp_dq = jnp.einsum(
        "dj,drkh->jrkh", picker, ret_dq, preferred_element_type=jnp.float32
    ).astype(jnp.bfloat16)[None, None]
    resp_dkv = jnp.einsum(
        "dj,dcrh->cjrh", picker, ret_kv, preferred_element_type=jnp.float32
    ).astype(jnp.bfloat16)[:, None, None]
    prompt_out = p_out.reshape(1, block_rows, kv_heads, local_width)
    prompt_dq = p_dq.astype(jnp.bfloat16).reshape(1, block_rows, kv_heads, local_width)
    return (prompt_out, prompt_dq, prompt_dkv, resp_out, resp_dq, resp_dkv)


def solution(mesh):
    return jax.shard_map(
        body,
        mesh=mesh,
        in_specs=(
            P("resp", "prompt", None, "head"),
            P(None, "resp", "prompt", None),
            P("resp", "prompt", None, "head"),
            P("prompt", "resp", None, None, None, "head"),
            P(None, "prompt", "resp", None, None, None),
            P("prompt", "resp", None, None, None, "head"),
            P("prompt", "resp", None),
        ),
        out_specs=(
            P("resp", "prompt", None, "head"),
            P("resp", "prompt", None, "head"),
            P(None, "resp", "prompt", "head"),
            P("prompt", "resp", None, None, None, "head"),
            P("prompt", "resp", None, None, None, "head"),
            P(None, "prompt", "resp", None, None, "head"),
        ),
        check_vma=False,
    )
```

profile of v0, /device:TPU:32, one launch (start us, length us, event | category | flops | bytes accessed | tf_op | source)
XLA Modules:
  0.0 611.9 jit_solution(9560362812889377372)
XLA Ops:
  11.9 5.5 all-to-all-start
  23.7 75.3 %all-gather.2.cloned.1.call-done = bf16[2,1,1024,512]{3,0,1,2:T(2,128)(2,1)} async-done(((bf16[2,1,64,512]{3,0,1,2:T(2,128)(2,1)}), bf16[2,1,1024,512]{3,0,1,2:T(2,128)(2,1)}) %all-gather.2.cloned.1.call-update) | async-done | bytes 2097168 | tf_op jit(solution)/shard_map/all_gather | solution.py:57
  99.0 6.5 %fusion.60 = (bf16[1,1,1024,512]{3,0,1,2:T(2,128)(2,1)S(1)}, bf16[1,1,1024,512]{3,0,1,2:T(2,128)(2,1)}) fusion(bf16[2,1,1024,512]{3,0,1,2:T(2,128)(2,1)} %all-gather.2.cloned.1.call-done), kind=kLoop, calls=%fused_computation.95 | loop fusion | bytes 4194304 | tf_op jit(solution)/shard_map/slice | solution.py:58
  105.5 2.6 copy.167
  108.1 4.3 all-to-all-start.1
  114.3 4.6 copy.168
  118.9 2.2 exponential_reduce_fusion.1
  123.5 5.1 all-to-all-start.2
  128.8 2.2 fusion.29
  134.3 2.3 pad_maximum_fusion.1
  136.6 4.2 all-to-all-done.2
  140.7 218.0 %while.16 = (s32[]{:T(128)}, f32[2,1024,4,128]{3,1,2,0:T(8,128)}, bf16[8,64,4,256]{3,2,1,0:T(4,128)(2,1)}, bf16[8,64,4,256]{3,2,1,0:T(4,128)(2,1)}, f32[8,2,64,5...) while((s32[]{:T(128)}, f32[2,1024,4,128]{3,1,2,0:T(8,128)}, ...), condition=%wide.region_5.6_spmd, body=%wide.region_2.5_spmd.sunk | while | flops 874970112 | bytes 124414592 | solution.py:116
  156.6 2.0 convolution_bitcast_fusion.5
  164.2 2.0 copy-done.3
  183.8 2.0 convolution_bitcast_fusion.5
  191.4 2.0 copy-done.3
  211.1 2.0 convolution_bitcast_fusion.5
  218.6 2.0 copy-done.3
  238.3 2.0 convolution_bitcast_fusion.5
  245.9 2.0 copy-done.3
  265.6 2.0 convolution_bitcast_fusion.5
  273.2 2.0 copy-done.3
  292.9 2.0 convolution_bitcast_fusion.5
  300.4 2.0 copy-done.3
  320.1 2.0 convolution_bitcast_fusion.5
  347.3 2.0 convolution_bitcast_fusion.5
  358.8 4.8 copy_bitcast_fusion.1
  364.8 18.6 %all_to_all.30 = bf16[8,64,4,256]{3,2,1,0:T(4,128)(2,1)} all-to-all(bf16[8,64,4,256]{3,2,1,0:T(4,128)(2,1)S(1)} %copy-done.22), channel_id=1, replica_groups=mesh['prompt'=16,'resp'=8,'head'=2] {'resp'}, dimensions={0} | all-to-all | bytes 2097152 | tf_op jit(solution)/shard_map/all_to_all | solution.py:126
  383.4 3.7 all-to-all-start.4
  387.1 2.1 convert_element_type.98
  389.2 199.5 %reduce-scatter.4.cloned.1.call-done = f32[2,64,512]{2,1,0:T(8,128)} async-done(((f32[2,1024,512]{2,1,0:T(8,128)}), f32[2,64,512]{2,1,0:T(8,128)}) %reduce-scatter.4.cloned.1.call-update) | async-done | bytes 262160 | tf_op jit(solution)/shard_map/reduce_scatter | solution.py:118
  588.7 4.4 all-to-all-start.5
  (571 shorter events, 220.2 us)
Async XLA Ops:
  7.2 91.8 %all-gather.2.cloned.1.call-start = ((), (), s32[]{:S(2)}) async-start(), calls=%async_computation.9 | async-start | bytes 2228224 | tf_op jit(solution)/shard_map/all_gather | solution.py:57
  10.5 7.1 %copy-start.20 = (bf16[2,1,1,8,64,512]{5,4,3,2,1,0:T(8,128)(2,1)S(1)}, bf16[2,1,1,8,64,512]{5,4,3,2,1,0:T(8,128)(2,1)}, u32[]{:S(2)}) copy-start(bf16[2,1,1,8,64,512]{5,4,3,2,1,0:T(8,128)(2,1)} %param.13) | copy-start | bytes 3145732
  10.5 7.0 %copy-start.25 = (s32[1,1,8]{2,1,0:T(1,128)S(1)}, s32[1,1,8]{2,1,0:T(1,128)}, u32[]{:S(2)}) copy-start(s32[1,1,8]{2,1,0:T(1,128)} %param.15) | copy-start | bytes 100
  11.9 6.5 %copy-start.21 = (bf16[1,1,8,64,4,256]{5,4,3,2,1,0:T(4,128)(2,1)S(1)}, bf16[1,1,8,64,4,256]{5,4,3,2,1,0:T(4,128)(2,1)}, u32[]{:S(2)}) copy-start(bf16[1,1,8,64,4,256]{5,4,3,2,1,0:T(4,128)(2,1)} %param.14) | copy-start | bytes 3145732
  11.9 96.2 %all-to-all-start = ((bf16[8,64,4,256]{3,2,1,0:T(4,128)(2,1)}), bf16[8,64,4,256]{3,2,1,0:T(4,128)(2,1)}, u32[]{:S(2)}, u32[]{:S(2)}) async-start(bf16[8,64,4,256]{3,2,1,0:T(4,128)(2,1)} %copy.99), calls=%async_computation | async-start | bytes 2097152 | tf_op jit(solution)/shard_map/all_to_all | solution.py:78
  108.1 15.4 %all-to-all-start.1 = ((bf16[8,2,64,512]{3,2,1,0:T(8,128)(2,1)}), bf16[8,2,64,512]{3,2,1,0:T(8,128)(2,1)}, u32[]{:S(2)}, u32[]{:S(2)}) async-start(bf16[8,2,64,512]{3,2,1,0:T(8,128)(2,1)} %copy.102), calls=%async_computation.1 | async-start | bytes 2097152 | tf_op jit(solution)/shard_map/all_to_all | solution.py:79
  123.5 17.2 %all-to-all-start.2 = ((bf16[8,64,4,256]{3,2,1,0:T(4,128)(2,1)}), bf16[8,64,4,256]{3,2,1,0:T(4,128)(2,1)}, u32[]{:S(2)}, u32[]{:S(2)}) async-start(bf16[8,64,4,256]{3,2,1,0:T(4,128)(2,1)} %copy.105), calls=%async_computation.2 | async-start | bytes 2097152 | tf_op jit(solution)/shard_map/all_to_all | solution.py:80
  128.6 258.5 %reduce-scatter.8.cloned.1.call-start = ((), (), s32[]{:S(2)}) async-start(), calls=%async_computation.12 | async-start | bytes 3145728 | tf_op jit(solution)/shard_map/reduce_scatter | solution.py:121
  140.7 5.8 copy-start.6
  140.7 7.1 %copy-start.8 = (bf16[1,1,1024,512]{2,3,1,0:T(8,128)(2,1)}, bf16[1,1,1024,512]{2,3,1,0:T(8,128)(2,1)S(1)}, u32[]{:S(2)}) copy-start(bf16[1,1,1024,512]{2,3,1,0:T(8,128)(2,1)S(1)} %get-tuple-element.277) | copy-start | bytes 3145732 | tf_op jit(solution)/shard_map/while
  167.9 5.8 copy-start.6
  167.9 7.2 %copy-start.8 = (bf16[1,1,1024,512]{2,3,1,0:T(8,128)(2,1)}, bf16[1,1,1024,512]{2,3,1,0:T(8,128)(2,1)S(1)}, u32[]{:S(2)}) copy-start(bf16[1,1,1024,512]{2,3,1,0:T(8,128)(2,1)S(1)} %get-tuple-element.277) | copy-start | bytes 3145732 | tf_op jit(solution)/shard_map/while
  195.2 5.8 copy-start.6
  195.2 7.2 %copy-start.8 = (bf16[1,1,1024,512]{2,3,1,0:T(8,128)(2,1)}, bf16[1,1,1024,512]{2,3,1,0:T(8,128)(2,1)S(1)}, u32[]{:S(2)}) copy-start(bf16[1,1,1024,512]{2,3,1,0:T(8,128)(2,1)S(1)} %get-tuple-element.277) | copy-start | bytes 3145732 | tf_op jit(solution)/shard_map/while
  218.6 3.8 copy-start.9
  222.5 5.8 copy-start.6
  222.5 7.2 %copy-start.8 = (bf16[1,1,1024,512]{2,3,1,0:T(8,128)(2,1)}, bf16[1,1,1024,512]{2,3,1,0:T(8,128)(2,1)S(1)}, u32[]{:S(2)}) copy-start(bf16[1,1,1024,512]{2,3,1,0:T(8,128)(2,1)S(1)} %get-tuple-element.277) | copy-start | bytes 3145732 | tf_op jit(solution)/shard_map/while
  249.7 5.8 copy-start.6
  249.7 7.2 %copy-start.8 = (bf16[1,1,1024,512]{2,3,1,0:T(8,128)(2,1)}, bf16[1,1,1024,512]{2,3,1,0:T(8,128)(2,1)S(1)}, u32[]{:S(2)}) copy-start(bf16[1,1,1024,512]{2,3,1,0:T(8,128)(2,1)S(1)} %get-tuple-element.277) | copy-start | bytes 3145732 | tf_op jit(solution)/shard_map/while
  277.0 5.8 copy-start.6
  277.0 7.2 %copy-start.8 = (bf16[1,1,1024,512]{2,3,1,0:T(8,128)(2,1)}, bf16[1,1,1024,512]{2,3,1,0:T(8,128)(2,1)S(1)}, u32[]{:S(2)}) copy-start(bf16[1,1,1024,512]{2,3,1,0:T(8,128)(2,1)S(1)} %get-tuple-element.277) | copy-start | bytes 3145732 | tf_op jit(solution)/shard_map/while
  304.2 5.8 copy-start.6
  304.2 7.2 %copy-start.8 = (bf16[1,1,1024,512]{2,3,1,0:T(8,128)(2,1)}, bf16[1,1,1024,512]{2,3,1,0:T(8,128)(2,1)S(1)}, u32[]{:S(2)}) copy-start(bf16[1,1,1024,512]{2,3,1,0:T(8,128)(2,1)S(1)} %get-tuple-element.277) | copy-start | bytes 3145732 | tf_op jit(solution)/shard_map/while
  331.5 5.8 copy-start.6
  331.5 7.2 %copy-start.8 = (bf16[1,1,1024,512]{2,3,1,0:T(8,128)(2,1)}, bf16[1,1,1024,512]{2,3,1,0:T(8,128)(2,1)S(1)}, u32[]{:S(2)}) copy-start(bf16[1,1,1024,512]{2,3,1,0:T(8,128)(2,1)S(1)} %get-tuple-element.277) | copy-start | bytes 3145732 | tf_op jit(solution)/shard_map/while
  358.7 230.0 %reduce-scatter.4.cloned.1.call-start = ((), (), s32[]{:S(2)}) async-start(), calls=%async_computation.10 | async-start | bytes 4456448 | tf_op jit(solution)/shard_map/reduce_scatter | solution.py:118
  383.4 209.7 %copy-start.18 = (bf16[4,2,64,1024]{3,2,1,0:T(8,128)(2,1)S(1)}, bf16[4,2,64,1024]{3,2,1,0:T(8,128)(2,1)}, u32[]{:S(2)}) copy-start(bf16[4,2,64,1024]{3,2,1,0:T(8,128)(2,1)} %copy-done.17) | copy-start | bytes 3145732
  383.4 205.3 %all-to-all-start.4 = ((bf16[8,64,4,256]{3,2,1,0:T(4,128)(2,1)}), bf16[8,64,4,256]{3,2,1,0:T(4,128)(2,1)S(1)}, u32[]{:S(2)}, u32[]{:S(2)}) async-start(bf16[8,64,4,256]{3,2,1,0:T(4,128)(2,1)} %get-tuple-element.68), calls=%async_computation.6 | async-start | bytes 2097152 | tf_op jit(solution)/shard_map/all_to_all | solution.py:127
  387.1 216.7 %reduce-scatter.6.cloned.1.call-start = ((), (), s32[]{:S(2)}) async-start(), calls=%async_computation.11 | async-start | bytes 393216 | tf_op jit(solution)/shard_map/reduce_scatter | solution.py:120
  389.2 204.3 %copy-start.23 = (bf16[4,2,64,128]{3,2,1,0:T(8,128)(2,1)S(1)}, bf16[4,2,64,128]{3,2,1,0:T(8,128)(2,1)}, u32[]{:S(2)}) copy-start(bf16[4,2,64,128]{3,2,1,0:T(8,128)(2,1)} %get-tuple-element.156) | copy-start | bytes 393220
  588.7 12.7 %all-to-all-start.5 = ((bf16[8,2,64,256]{3,2,1,0:T(8,128)(2,1)}), bf16[8,2,64,256]{3,2,1,0:T(8,128)(2,1)}, u32[]{:S(2)}, u32[]{:S(2)}) async-start(bf16[8,2,64,256]{3,2,1,0:T(8,128)(2,1)} %convert_element_type.98), calls=%async_computation.8 | async-start | bytes 1048576 | tf_op jit(solution)/shard_map/all_to_all | solution.py:128
  598.7 6.7 %copy-start.1 = (bf16[1,1,8,64,4,256]{5,4,3,2,1,0:T(4,128)(2,1)S(1)}, bf16[1,1,8,64,4,256]{5,4,3,2,1,0:T(4,128)(2,1)}, u32[]{:S(2)}) copy-start(bf16[1,1,8,64,4,256]{5,4,3,2,1,0:T(4,128)(2,1)} %param.12) | copy-start | bytes 3145732
  (117 other events, 216.3 us)
Sparse Core Ops, SparseCore 0:
  11.2 87.7 all-gather.1
  358.9 13.8 reduce-scatter.7
  377.3 211.3 reduce-scatter.3
  591.0 12.0 reduce-scatter.5
where the time goes:
time: 616 us; the launch traced here: 612 us
  waiting for transfers between devices  280 us (45%)
  local copies, waits for them, and re-layouts  175 us (28%)
  matrix products  71.7 us (12%)
  other arithmetic  26.9 us (4%)
  starting transfers between devices  23.3 us (4%)
  blocking collectives  18.6 us (3%)
  between operations  14.1 us (2%)
    reduce_scatter x1, waiting for transfers between devices, body(): lax.psum_scatter(prompt_part, 'prompt', scatter_dimension=1, tiled=True)  199 us
    all_gather x1, waiting for transfers between devices, body(): gathered = lax.all_gather(prompt_kv, 'prompt', axis=2, tiled=True)  75.3 us
    while x224, local copies, waits for them, and re-layouts  41.1 us
    dynamic_update_slice x48, local copies, waits for them, and re-layouts, body(): lax.scan(one_response, start, (got_q, got_kv, got_grad))  33.5 us
    all_to_all x1, blocking collectives, body(): lax.all_to_all(back_out, 'resp', split_axis=0, concat_axis=0, tiled=True)  18.6 us
    unnamed x34, local copies, waits for them, and re-layouts  17.6 us
    dot_general x9, matrix products, attend(): jnp.einsum('brkgd,bnkd->bkgrn', queries, keys_in, preferred_element_type=...  17.6 us
    dot_general x9, matrix products, attend(): jnp.einsum('bkgrn,brkgd->bnkd', weights, cotangent, preferred_element_typ...  17 us
  transfers between devices with their start and end apart: 9, of which 5 were waited for; matrix products, arithmetic and copies ran while one was open for 8% of the time, Pallas kernels for 0%

commit v1 on v0

v1 whole, which is shorter than its diff:
```python
import math

import jax
import jax.numpy as jnp
from jax import lax
from jax.sharding import PartitionSpec as P

HD = 128


def attend_blocks(queries, keys_in, values_in, own_keys, own_values, cotangent, shared_ok, own_ok):
    scale = 1.0 / math.sqrt(HD)
    f32 = jnp.float32
    s_sh = jnp.einsum("brkgd,nkd->bkgrn", queries, keys_in, preferred_element_type=f32) * scale
    s_own = jnp.einsum("brkgd,bukd->bkgru", queries, own_keys, preferred_element_type=f32) * scale
    s_sh = jnp.where(shared_ok[:, None, None], s_sh, -1e30)
    s_own = jnp.where(own_ok[:, None, None], s_own, -1e30)
    row_max = jnp.maximum(
        jnp.max(s_sh, axis=-1, keepdims=True), jnp.max(s_own, axis=-1, keepdims=True)
    )
    totals = jnp.sum(jnp.exp(s_sh - row_max), axis=-1, keepdims=True) + jnp.sum(
        jnp.exp(s_own - row_max), axis=-1, keepdims=True
    )
    log_total = row_max + jnp.log(totals)
    p_sh = jnp.exp(s_sh - log_total)
    p_own = jnp.exp(s_own - log_total)
    w_sh = p_sh.astype(jnp.bfloat16)
    w_own = p_own.astype(jnp.bfloat16)
    output = (
        jnp.einsum("bkgrn,nkd->brkgd", w_sh, values_in, preferred_element_type=f32)
        + jnp.einsum("bkgru,bukd->brkgd", w_own, own_values, preferred_element_type=f32)
    ).astype(jnp.bfloat16)
    row_delta = jnp.einsum("brkgd,brkgd->bkgr", cotangent, output, preferred_element_type=f32)
    dp_sh = jnp.einsum("brkgd,nkd->bkgrn", cotangent, values_in, preferred_element_type=f32)
    dp_own = jnp.einsum("brkgd,bukd->bkgru", cotangent, own_values, preferred_element_type=f32)
    ds_sh = (p_sh * (dp_sh - row_delta[..., None])).astype(jnp.bfloat16)
    ds_own = (p_own * (dp_own - row_delta[..., None])).astype(jnp.bfloat16)
    dquery = (
        jnp.einsum("bkgrn,nkd->brkgd", ds_sh, keys_in, preferred_element_type=f32)
        + jnp.einsum("bkgru,bukd->brkgd", ds_own, own_keys, preferred_element_type=f32)
    ) * scale
    dk_sh = jnp.einsum("bkgrn,brkgd->nkd", ds_sh, queries, preferred_element_type=f32) * scale
    dv_sh = jnp.einsum("bkgrn,brkgd->nkd", w_sh, cotangent, preferred_element_type=f32)
    dk_own = jnp.einsum("bkgru,brkgd->bukd", ds_own, queries, preferred_element_type=f32) * scale
    dv_own = jnp.einsum("bkgru,brkgd->bukd", w_own, cotangent, preferred_element_type=f32)
    return output, dquery, dk_sh, dv_sh, dk_own, dv_own


def body(prompt_q, prompt_kv, prompt_grad, resp_q, resp_kv, resp_grad, resp_prompt):
    head_size = HD
    block_rows = prompt_q.shape[1]
    kv_heads = prompt_q.shape[2]
    local_width = prompt_q.shape[3]
    local_heads = local_width // head_size
    full_len = block_rows * lax.axis_size("prompt")
    resp_len = resp_q.shape[3]
    peers = lax.axis_size("resp")
    kv_width = kv_heads * head_size
    gathered = lax.all_gather(prompt_kv, "prompt", axis=2, tiled=True)
    prompt_keys = gathered[0, 0].reshape(full_len, kv_heads, head_size)
    prompt_values = gathered[1, 0].reshape(full_len, kv_heads, head_size)

    order = resp_prompt[0, 0]
    picker = (jnp.arange(peers)[:, None] == order[None, :]).astype(jnp.bfloat16)
    send_q = jnp.einsum(
        "dj,jrkh->drkh", picker, resp_q[0, 0], preferred_element_type=jnp.float32
    ).astype(jnp.bfloat16)
    send_kv = jnp.einsum(
        "dj,cjrh->dcrh", picker, resp_kv[:, 0, 0], preferred_element_type=jnp.float32
    ).astype(jnp.bfloat16)
    send_grad = jnp.einsum(
        "dj,jrkh->drkh", picker, resp_grad[0, 0], preferred_element_type=jnp.float32
    ).astype(jnp.bfloat16)
    got_q, got_kv, got_grad = (
        lax.all_to_all(send_q, "resp", split_axis=0, concat_axis=0, tiled=True),
        lax.all_to_all(send_kv, "resp", split_axis=0, concat_axis=0, tiled=True),
        lax.all_to_all(send_grad, "resp", split_axis=0, concat_axis=0, tiled=True),
    )

    q_shape = (peers + 1, resp_len, kv_heads, local_heads, head_size)
    queries = jnp.concatenate([got_q, prompt_q], axis=0).reshape(q_shape)
    cotangent = jnp.concatenate([got_grad, prompt_grad], axis=0).reshape(q_shape)
    own_kv = jnp.concatenate(
        [got_kv, jnp.zeros((1,) + got_kv.shape[1:], got_kv.dtype)], axis=0
    ).reshape(peers + 1, 2, resp_len, kv_heads, head_size)
    query_rows = lax.axis_index("prompt") * block_rows + jnp.arange(block_rows)
    key_cols = jnp.arange(full_len)
    causal = key_cols[None, :] <= query_rows[:, None]
    shared_ok = jnp.concatenate(
        [jnp.ones((peers, resp_len, full_len), bool), causal[None]], axis=0
    )
    steps_own = jnp.arange(resp_len)
    own_causal = steps_own[None, :] <= steps_own[:, None]
    own_ok = jnp.concatenate(
        [
            jnp.broadcast_to(own_causal, (peers, resp_len, resp_len)),
            jnp.zeros((1, resp_len, resp_len), bool),
        ],
        axis=0,
    )
    out, dq, dk_sh, dv_sh, dk_own, dv_own = attend_blocks(
        queries,
        prompt_keys,
        prompt_values,
        own_kv[:, 0],
        own_kv[:, 1],
        cotangent,
        shared_ok,
        own_ok,
    )
    out = out.reshape(peers + 1, resp_len, kv_heads, local_width)
    dq = dq.astype(jnp.bfloat16).reshape(peers + 1, resp_len, kv_heads, local_width)

    prompt_part = jnp.stack([dk_sh, dv_sh]).reshape(2, full_len, kv_width)
    head_sum = lax.psum_scatter(prompt_part, "head", scatter_dimension=2, tiled=True)
    block_sum = lax.psum_scatter(head_sum, "prompt", scatter_dimension=1, tiled=True)
    own_part = jnp.stack([dk_own[:peers], dv_own[:peers]], axis=1).reshape(
        peers, 2, resp_len, kv_width
    )
    own_sum = lax.psum_scatter(own_part, "head", scatter_dimension=3, tiled=True)
    prompt_dkv = block_sum.astype(jnp.bfloat16)[:, None]
    back_kv = own_sum.astype(jnp.bfloat16)
    ret_out, ret_dq, ret_kv = (
        lax.all_to_all(out[:peers], "resp", split_axis=0, concat_axis=0, tiled=True),
        lax.all_to_all(dq[:peers], "resp", split_axis=0, concat_axis=0, tiled=True),
        lax.all_to_all(back_kv, "resp", split_axis=0, concat_axis=0, tiled=True),
    )
    resp_out = jnp.einsum(
        "dj,drkh->jrkh", picker, ret_out, preferred_element_type=jnp.float32
    ).astype(jnp.bfloat16)[None, None]
    resp_dq = jnp.einsum(
        "dj,drkh->jrkh", picker, ret_dq, preferred_element_type=jnp.float32
    ).astype(jnp.bfloat16)[None, None]
    resp_dkv = jnp.einsum(
        "dj,dcrh->cjrh", picker, ret_kv, preferred_element_type=jnp.float32
    ).astype(jnp.bfloat16)[:, None, None]
    prompt_out = out[peers:]
    prompt_dq = dq[peers:]
    return (prompt_out, prompt_dq, prompt_dkv, resp_out, resp_dq, resp_dkv)


def solution(mesh):
    return jax.shard_map(
        body,
        mesh=mesh,
        in_specs=(
            P("resp", "prompt", None, "head"),
            P(None, "resp", "prompt", None),
            P("resp", "prompt", None, "head"),
            P("prompt", "resp", None, None, None, "head"),
            P(None, "prompt", "resp", None, None, None),
            P("prompt", "resp", None, None, None, "head"),
            P("prompt", "resp", None),
        ),
        out_specs=(
            P("resp", "prompt", None, "head"),
            P("resp", "prompt", None, "head"),
            P(None, "resp", "prompt", "head"),
            P("prompt", "resp", None, None, None, "head"),
            P("prompt", "resp", None, None, None, "head"),
            P(None, "prompt", "resp", None, None, "head"),
        ),
        check_vma=False,
    )
```

time: 616 us -> 440 us (0.71)
  local copies, waits for them, and re-layouts: 175 us -> 60 us
  waiting for transfers between devices: 280 us -> 248 us
  blocking collectives: 18.6 us -> 0 us
  matrix products: 71.7 us -> 61.5 us
    all_gather x1, waiting for transfers between devices: 75.3 us -> 19.4 us  [body(): gathered = lax.all_gather(prompt_kv, 'prompt', axis=2, tiled=True)]
    while x224 -> x0, local copies, waits for them, and re-layouts: 41.1 us -> none
    reduce_scatter x2, waiting for transfers between devices: 199 us -> 162 us  [the longest x1 161 us: body(): lax.psum_scatter(head_sum, 'prompt', scatter_dimension=1, tiled=True)]
    dynamic_update_slice x48 -> x0, local copies, waits for them, and re-layouts: 33.5 us -> none  [body(): lax.scan(one_response, start, (got_q, got_kv, got_grad))]
    all_to_all x1 -> x2, waiting for transfers between devices: 0.01 us -> 25.9 us  [the longest x1 13.5 us: body(): lax.all_to_all(out[:peers], 'resp', split_axis=0, concat_axis=0, tiled=True)]
    all_to_all x1 -> x0, blocking collectives: 18.6 us -> none  [body(): lax.all_to_all(back_out, 'resp', split_axis=0, concat_axis=0, tiled=True)]
    another operation x42 -> x4, local copies, waits for them, and re-layouts: 24.3 us -> 7.9 us  [the longest x2 4.85 us: body(): prompt_part = jnp.stack([dk_sh, dv_sh]).reshape(2, full_len, kv_width)]
    dynamic_slice x16 -> x0, local copies, waits for them, and re-layouts: 15.3 us -> none  [body(): lax.scan(one_response, start, (got_q, got_kv, got_grad))]
  transfers between devices with their start and end apart: 9 -> 10, of which waited for: 5 -> 9; matrix products, arithmetic and copies ran while one was open for 8% -> 13% of each run, Pallas kernels for 0% -> 0%
where the time goes in v1:
time: 440 us; the launch traced here: 433 us
  waiting for transfers between devices  248 us (56%)
  matrix products  61.5 us (14%)
  local copies, waits for them, and re-layouts  60 us (14%)
  starting transfers between devices  27.4 us (6%)
  other arithmetic  21.2 us (5%)
  between operations  14.5 us (3%)
    reduce_scatter x1, waiting for transfers between devices, body(): lax.psum_scatter(head_sum, 'prompt', scatter_dimension=1, tiled=True)  161 us
    unnamed x64, local copies, waits for them, and re-layouts  24.6 us
    all_gather x1, waiting for transfers between devices, body(): gathered = lax.all_gather(prompt_kv, 'prompt', axis=2, tiled=True)  19.4 us
    all_to_all x1, waiting for transfers between devices, body(): lax.all_to_all(out[:peers], 'resp', split_axis=0, concat_axis=0, tiled=True)  13.5 us
    all_to_all x1, waiting for transfers between devices, body(): lax.all_to_all(send_grad, 'resp', split_axis=0, concat_axis=0, tiled=True)  13.2 us
    all_to_all x1, waiting for transfers between devices, body(): lax.all_to_all(send_q, 'resp', split_axis=0, concat_axis=0, tiled=True)  12.9 us
    all_to_all x1, waiting for transfers between devices, body(): lax.all_to_all(dq[:peers], 'resp', split_axis=0, concat_axis=0, tiled=True)  12.5 us
    all_to_all x1, waiting for transfers between devices, body(): lax.all_to_all(send_kv, 'resp', split_axis=0, concat_axis=0, tiled=True)  11.9 us
  transfers between devices with their start and end apart: 10, of which 9 were waited for; matrix products, arithmetic and copies ran while one was open for 13% of the time, Pallas kernels for 0%

profile of v1, /device:TPU:32, one launch (start us, length us, event | category | flops | bytes accessed | tf_op | source)
XLA Modules:
  0.0 432.5 jit_solution(9284214201687019022)
XLA Ops:
  11.9 5.4 %all-to-all-start = ((bf16[8,64,4,256]{3,2,1,0:T(4,128)(2,1)}), bf16[8,64,4,256]{3,2,1,0:T(4,128)(2,1)S(1)}, u32[]{:S(2)}, u32[]{:S(2)}) async-start(bf16[8,64,4,256]{3,2,1,0:T(4,128)(2,1)} %copy.205), calls=%async_computation | async-start | bytes 2097152 | tf_op jit(solution)/shard_map/all_to_all | solution.py:75
  19.4 12.9 %all-to-all-done = bf16[8,64,4,256]{3,2,1,0:T(4,128)(2,1)S(1)} async-done(((bf16[8,64,4,256]{3,2,1,0:T(4,128)(2,1)}), bf16[8,64,4,256]{3,2,1,0:T(4,128)(2,1)S(1)}, u32[]{:S(2)}, u32[]{:S(2)}) %all-to-all-start) | async-done | bytes 1048608 | tf_op jit(solution)/shard_map/all_to_all | solution.py:75
  32.3 4.2 all-to-all-start.1
  38.8 11.9 %all-to-all-done.1 = bf16[8,2,64,512]{3,2,1,0:T(8,128)(2,1)S(1)} async-done(((bf16[8,2,64,512]{3,2,1,0:T(8,128)(2,1)}), bf16[8,2,64,512]{3,2,1,0:T(8,128)(2,1)S(1)}, u32[]{:S(2)}, u32[]{:S(2)}) %all-to-all-start.1) | async-done | bytes 1048608 | tf_op jit(solution)/shard_map/all_to_all | solution.py:76
  50.7 4.2 all-to-all-start.2
  59.5 13.2 %all-to-all-done.2 = bf16[8,64,4,256]{3,2,1,0:T(4,128)(2,1)} async-done(((bf16[8,64,4,256]{3,2,1,0:T(4,128)(2,1)}), bf16[8,64,4,256]{3,2,1,0:T(4,128)(2,1)}, u32[]{:S(2)}, u32[]{:S(2)}) %all-to-all-start.2) | async-done | bytes 1048608 | tf_op jit(solution)/shard_map/all_to_all | solution.py:77
  72.8 3.0 pad_maximum_fusion.3
  75.8 2.8 reshape.118
  79.2 2.7 copy_convert_fusion
  83.2 19.4 %all-gather.2.cloned.1.call-done = bf16[2,1,1024,512]{3,0,1,2:T(2,128)(2,1)} async-done(((bf16[2,1,64,512]{3,0,1,2:T(2,128)(2,1)}), bf16[2,1,1024,512]{3,0,1,2:T(2,128)(2,1)}) %all-gather.2.cloned.1.call-update) | async-done | bytes 2097168 | tf_op jit(solution)/shard_map/all_gather | solution.py:59
  102.5 6.9 %fusion.60 = (bf16[1,1,1024,512]{3,0,1,2:T(2,128)(2,1)}, bf16[1,1,1024,512]{3,0,1,2:T(2,128)(2,1)}) fusion(bf16[2,1,1024,512]{3,0,1,2:T(2,128)(2,1)} %all-gather.2.cloned.1.call-done), kind=kLoop, calls=%fused_computation.87 | loop fusion | bytes 4194304 | tf_op jit(solution)/shard_map/slice | solution.py:61
  109.4 5.8 %copy.323 = bf16[1,1,1024,512]{2,3,1,0:T(8,128)(2,1)} copy(bf16[1,1,1024,512]{3,0,1,2:T(2,128)(2,1)} %get-tuple-element.37) | data formatting | bytes 2097152
  115.3 5.6 %bitcast_reduce_fusion = (f32[9,4,2,64]{3,2,0,1:T(2,128)S(1)}, f32[4,9,64,2,1024]{4,2,3,1,0:T(8,128)S(1)}) fusion(pred[9,64,1024]{2,1,0:T(8,128)(4,1)} %concatenate.17, bf16[1024,4,128,1,1]{0,2,4,3,1:T(8,128)(2,1)} %bitcast.155, bf16[9,64,4,2,128]{4,3,2,1,0:T(2,128)(2,1)} %reshape.116), kind=kOutput, calls=%fused_computation.5 | convolution fusion | flops 1222110720 | bytes 21710848 | tf_op jit(solution)/shard_map/brkgd,nkd->bkgrn/dot_general | solution.py:14
  121.0 5.4 %fusion.3 = f32[9,4,2,64]{3,2,0,1:T(2,128)S(1)} fusion(f32[4,9,64,2,1024]{4,2,3,1,0:T(8,128)S(1)} %get-tuple-element.43, f32[9,4,2,64]{3,2,0,1:T(2,128)S(1)} %copy.218, pred[9,64,1024]{2,1,0:T(8,128)(4,1)S(1)} %copy-done.13), kind=kLoop, calls=%fused_computation.7 | loop fusion | flops 18869760 | bytes 19501056 | tf_op jit(solution)/shard_map/reduce_sum | solution.py:21
  128.0 5.8 %copy.325 = bf16[1,1,1024,512]{2,3,1,0:T(8,128)(2,1)} copy(bf16[1,1,1024,512]{3,0,1,2:T(2,128)(2,1)} %get-tuple-element.36) | data formatting | bytes 2097152
  133.9 10.9 %fusion.28 = f32[4,128,1024,1,1]{2,1,4,3,0:T(8,128)} fusion(bf16[9,64,4,2,128]{4,3,2,1,0:T(2,128)(2,1)} %copy-done.6, f32[4,9,64,2,1024]{4,2,3,1,0:T(8,128)} %copy-done.5, f32[9,4,2,64]{3,2,0,1:T(2,128)S(1)} %copy.222, pred[9,64,1024]{2,1,0:T(8,128)(4,1)} %concatenate.17), kind=kOutput, calls=%fused_computation.54 | convolution fusion | flops 1226833920 | bytes 22759424 | tf_op jit(solution)/shard_map/bkgrn,brkgd->nkd/dot_general | solution.py:43
  146.9 10.0 %multiply_reduce_fusion = (f32[9,4,2,64]{3,2,0,1:T(2,128)S(1)}, bf16[9,64,4,2,128]{4,1,3,0,2:T(8,128)(2,1)}) fusion(f32[9,4,2,64,128]{4,2,3,1,0:T(2,128)S(1)} %copy-done.16, f32[9,4,128,2,64]{2,4,3,0,1:T(8,128)S(1)} %fusion.19, bf16[1024,4,128,1,1]{0,2,4,3,1:T(8,128)(2,1)S(1)} %bitcast.159, f32[4,9,64,2,1024]{4,2,3,1,0:T(8,128)} %copy-done.5, ...), kind=kOutput, calls=%fused_computation.21 | convolution fusion | flops 1229778432 | bytes 26447872 | tf_op jit(solution)/shard_map/bkgrn,nkd->brkgd/dot_general | solution.py:30
  156.9 10.1 %fusion.1 = bf16[9,4,2,64,1024]{4,3,2,0,1:T(8,128)(2,1)S(1)} fusion(f32[4,9,64,2,1024]{4,2,3,1,0:T(8,128)} %copy-done.5, f32[9,4,2,64]{3,2,0,1:T(2,128)S(1)} %get-tuple-element.44, f32[9,4,2,64]{3,2,0,1:T(2,128)S(1)} %copy.222, pred[9,64,1024]{2,1,0:T(8,128)(4,1)S(1)} %copy-done.15, bf16[1024,4,128,1,1]{0,2,4,3,1:T(8,128)(2,1)} %bitcast.158, ...), kind=kOutput, calls=%fused_computation.2 | convolution fusion | flops 1236271104 | bytes 31166464 | tf_op jit(solution)/shard_map/brkgd,nkd->bkgrn/dot_general | solution.py:34
  167.0 5.2 %bitcast_multiply_fusion = f32[4,128,1024]{2,1,0:T(8,128)} fusion(bf16[9,4,2,64,1024]{4,3,2,0,1:T(8,128)(2,1)S(1)} %fusion.1, bf16[9,64,4,2,128]{4,3,2,1,0:T(2,128)(2,1)} %reshape.116), kind=kOutput, calls=%fused_computation.25 | convolution fusion | flops 1208483840 | bytes 12713984 | tf_op jit(solution)/shard_map/bkgrn,brkgd->nkd/dot_general | solution.py:42
  172.2 1.9 copy.244
  174.2 2.9 copy.245
  177.1 4.1 pad_maximum_fusion
  186.5 2.6 stack.22
  189.1 2.6 fusion.9
  198.6 6.3 %fusion.7 = bf16[9,64,4,2,128]{4,1,3,0,2:T(8,128)(2,1)S(1)} fusion(f32[9,4,128,2,64]{2,4,3,0,1:T(8,128)S(1)} %fusion.17, bf16[9,4,2,64,1024]{4,3,2,0,1:T(8,128)(2,1)} %copy-done.2, bf16[1024,4,128,1,1]{0,2,4,3,1:T(8,128)(2,1)S(1)} %bitcast.156), kind=kOutput, calls=%fused_computation.14 | convolution fusion | flops 1209729024 | bytes 14024704 | tf_op jit(solution)/shard_map/bkgrn,nkd->brkgd/dot_general | solution.py:39
  207.5 4.9 %all-to-all-start.4 = ((bf16[8,64,4,256]{3,2,1,0:T(4,128)(2,1)}), bf16[8,64,4,256]{3,2,1,0:T(4,128)(2,1)S(1)}, u32[]{:S(2)}, u32[]{:S(2)}) async-start(bf16[8,64,4,256]{3,2,1,0:T(4,128)(2,1)} %reshape.121), calls=%async_computation.6 | async-start | bytes 2097152 | tf_op jit(solution)/shard_map/all_to_all | solution.py:125
  215.1 12.5 %all-to-all-done.4 = bf16[8,64,4,256]{3,2,1,0:T(4,128)(2,1)S(1)} async-done(((bf16[8,64,4,256]{3,2,1,0:T(4,128)(2,1)}), bf16[8,64,4,256]{3,2,1,0:T(4,128)(2,1)S(1)}, u32[]{:S(2)}, u32[]{:S(2)}) %all-to-all-start.4) | async-done | bytes 1048608 | tf_op jit(solution)/shard_map/all_to_all | solution.py:125
  227.6 3.6 all-to-all-start.3
  233.4 13.5 %all-to-all-done.3 = bf16[8,64,4,256]{3,2,1,0:T(4,128)(2,1)S(1)} async-done(((bf16[8,64,4,256]{3,2,1,0:T(4,128)(2,1)}), bf16[8,64,4,256]{3,2,1,0:T(4,128)(2,1)S(1)}, u32[]{:S(2)}, u32[]{:S(2)}) %all-to-all-start.3) | async-done | bytes 1048608 | tf_op jit(solution)/shard_map/all_to_all | solution.py:124
  246.8 4.6 %all-to-all-start.5 = ((bf16[8,2,64,256]{3,2,1,0:T(8,128)(2,1)}), bf16[8,2,64,256]{3,2,1,0:T(8,128)(2,1)}, u32[]{:S(2)}, u32[]{:S(2)}) async-start(bf16[8,2,64,256]{3,2,1,0:T(8,128)(2,1)} %copy.256), calls=%async_computation.8 | async-start | bytes 1048576 | tf_op jit(solution)/shard_map/all_to_all | solution.py:126
  258.4 2.2 all-to-all-done.5
  263.0 161.3 %reduce-scatter.6.cloned.1.call-done = f32[2,64,256]{2,1,0:T(8,128)} async-done(((f32[2,1024,256]{2,1,0:T(8,128)}), f32[2,64,256]{2,1,0:T(8,128)}) %reduce-scatter.6.cloned.1.call-update) | async-done | bytes 131088 | tf_op jit(solution)/shard_map/reduce_scatter | solution.py:116
  (121 shorter events, 49.4 us)
Async XLA Ops:
  7.2 1.9 copy-start
  7.2 95.3 %all-gather.2.cloned.1.call-start = ((), (), s32[]{:S(2)}) async-start(), calls=%async_computation.9 | async-start | bytes 2228224 | tf_op jit(solution)/shard_map/all_gather | solution.py:59
  10.5 6.8 %copy-start.21 = (bf16[2,1,1,8,64,512]{5,4,3,2,1,0:T(8,128)(2,1)S(1)}, bf16[2,1,1,8,64,512]{5,4,3,2,1,0:T(8,128)(2,1)}, u32[]{:S(2)}) copy-start(bf16[2,1,1,8,64,512]{5,4,3,2,1,0:T(8,128)(2,1)} %param.11) | copy-start | bytes 3145732
  10.5 6.8 %copy-start.26 = (s32[1,1,8]{2,1,0:T(1,128)S(1)}, s32[1,1,8]{2,1,0:T(1,128)}, u32[]{:S(2)}) copy-start(s32[1,1,8]{2,1,0:T(1,128)} %param.13) | copy-start | bytes 100
  11.9 20.4 %all-to-all-start = ((bf16[8,64,4,256]{3,2,1,0:T(4,128)(2,1)}), bf16[8,64,4,256]{3,2,1,0:T(4,128)(2,1)S(1)}, u32[]{:S(2)}, u32[]{:S(2)}) async-start(bf16[8,64,4,256]{3,2,1,0:T(4,128)(2,1)} %copy.205), calls=%async_computation | async-start | bytes 2097152 | tf_op jit(solution)/shard_map/all_to_all | solution.py:75
  18.1 18.5 %copy-start.22 = (bf16[1,1,8,64,4,256]{5,4,3,2,1,0:T(4,128)(2,1)S(1)}, bf16[1,1,8,64,4,256]{5,4,3,2,1,0:T(4,128)(2,1)}, u32[]{:S(2)}) copy-start(bf16[1,1,8,64,4,256]{5,4,3,2,1,0:T(4,128)(2,1)} %param.12) | copy-start | bytes 3145732
  32.3 18.4 %all-to-all-start.1 = ((bf16[8,2,64,512]{3,2,1,0:T(8,128)(2,1)}), bf16[8,2,64,512]{3,2,1,0:T(8,128)(2,1)S(1)}, u32[]{:S(2)}, u32[]{:S(2)}) async-start(bf16[8,2,64,512]{3,2,1,0:T(8,128)(2,1)} %copy.213), calls=%async_computation.1 | async-start | bytes 2097152 | tf_op jit(solution)/shard_map/all_to_all | solution.py:76
  37.4 19.4 %copy-start.23 = (bf16[1,64,4,256]{3,2,1,0:T(4,128)(2,1)S(1)}, bf16[1,64,4,256]{3,2,1,0:T(4,128)(2,1)}, u32[]{:S(2)}) copy-start(bf16[1,64,4,256]{3,2,1,0:T(4,128)(2,1)} %param.7) | copy-start | bytes 393220
  50.7 22.1 %all-to-all-start.2 = ((bf16[8,64,4,256]{3,2,1,0:T(4,128)(2,1)}), bf16[8,64,4,256]{3,2,1,0:T(4,128)(2,1)}, u32[]{:S(2)}, u32[]{:S(2)}) async-start(bf16[8,64,4,256]{3,2,1,0:T(4,128)(2,1)} %copy.231), calls=%async_computation.2 | async-start | bytes 2097152 | tf_op jit(solution)/shard_map/all_to_all | solution.py:77
  55.0 142.0 %reduce-scatter.4.cloned.1.call-start = ((), (), s32[]{:S(2)}) async-start(), calls=%async_computation.10 | async-start | bytes 6291456 | tf_op jit(solution)/shard_map/reduce_scatter | solution.py:115
  59.1 13.7 %copy-start.24 = (bf16[1,64,4,256]{3,2,1,0:T(4,128)(2,1)S(1)}, bf16[1,64,4,256]{3,2,1,0:T(4,128)(2,1)}, u32[]{:S(2)}) copy-start(bf16[1,64,4,256]{3,2,1,0:T(4,128)(2,1)} %param.9) | copy-start | bytes 393220
  78.6 3.2 copy-start.6
  79.2 2.7 copy-start.17
  79.2 2.7 copy-start.7
  79.2 2.7 copy-start.25
  83.2 61.6 %copy-start.3 = (f32[9,4,2,64,64]{3,4,2,1,0:T(8,128)}, f32[9,4,2,64,64]{3,4,2,1,0:T(8,128)S(1)}, u32[]{:S(2)}) copy-start(f32[9,4,2,64,64]{3,4,2,1,0:T(8,128)S(1)} %get-tuple-element.41) | copy-start | bytes 3538948
  115.3 5.7 %copy-start.13 = (pred[9,64,1024]{2,1,0:T(8,128)(4,1)S(1)}, pred[9,64,1024]{2,1,0:T(8,128)(4,1)}, u32[]{:S(2)}) copy-start(pred[9,64,1024]{2,1,0:T(8,128)(4,1)} %concatenate.17) | copy-start | bytes 1769476
  120.9 6.4 %copy-start.5 = (f32[4,9,64,2,1024]{4,2,3,1,0:T(8,128)}, f32[4,9,64,2,1024]{4,2,3,1,0:T(8,128)S(1)}, u32[]{:S(2)}) copy-start(f32[4,9,64,2,1024]{4,2,3,1,0:T(8,128)S(1)} %get-tuple-element.43) | copy-start | bytes 56623108
  144.8 1.9 copy-start.16
  144.8 2.1 copy-start.20
  146.9 10.0 %copy-start.15 = (pred[9,64,1024]{2,1,0:T(8,128)(4,1)S(1)}, pred[9,64,1024]{2,1,0:T(8,128)(4,1)}, u32[]{:S(2)}) copy-start(pred[9,64,1024]{2,1,0:T(8,128)(4,1)} %concatenate.17) | copy-start | bytes 1769476
  167.0 5.2 %copy-start.2 = (bf16[9,4,2,64,1024]{4,3,2,0,1:T(8,128)(2,1)}, bf16[9,4,2,64,1024]{4,3,2,0,1:T(8,128)(2,1)S(1)}, u32[]{:S(2)}) copy-start(bf16[9,4,2,64,1024]{4,3,2,0,1:T(8,128)(2,1)S(1)} %fusion.1) | copy-start | bytes 28311556
  181.2 1.7 copy-start.4
  181.2 50.0 %reduce-scatter.8.cloned.1.call-start = ((), (), s32[]{:S(2)}) async-start(), calls=%async_computation.12 | async-start | bytes 3145728 | tf_op jit(solution)/shard_map/reduce_scatter | solution.py:120
  189.1 2.6 copy-start.8
  195.8 1.5 copy-start.18
  195.8 228.4 %reduce-scatter.6.cloned.1.call-start = ((), (), s32[]{:S(2)}) async-start(), calls=%async_computation.11 | async-start | bytes 2228224 | tf_op jit(solution)/shard_map/reduce_scatter | solution.py:116
  206.0 6.4 %copy-start.19 = (bf16[9,64,4,2,128]{4,1,3,0,2:T(8,128)(2,1)S(1)}, bf16[9,64,4,2,128]{4,1,3,0,2:T(8,128)(2,1)}, u32[]{:S(2)}) copy-start(bf16[9,64,4,2,128]{4,1,3,0,2:T(8,128)(2,1)} %get-tuple-element.45) | copy-start | bytes 3538948
  207.5 20.0 %all-to-all-start.4 = ((bf16[8,64,4,256]{3,2,1,0:T(4,128)(2,1)}), bf16[8,64,4,256]{3,2,1,0:T(4,128)(2,1)S(1)}, u32[]{:S(2)}, u32[]{:S(2)}) async-start(bf16[8,64,4,256]{3,2,1,0:T(4,128)(2,1)} %reshape.121), calls=%async_computation.6 | async-start | bytes 2097152 | tf_op jit(solution)/shard_map/all_to_all | solution.py:125
  227.6 19.3 %all-to-all-start.3 = ((bf16[8,64,4,256]{3,2,1,0:T(4,128)(2,1)}), bf16[8,64,4,256]{3,2,1,0:T(4,128)(2,1)S(1)}, u32[]{:S(2)}, u32[]{:S(2)}) async-start(bf16[8,64,4,256]{3,2,1,0:T(4,128)(2,1)} %reshape.120), calls=%async_computation.5 | async-start | bytes 2097152 | tf_op jit(solution)/shard_map/all_to_all | solution.py:124
  246.8 13.8 %all-to-all-start.5 = ((bf16[8,2,64,256]{3,2,1,0:T(8,128)(2,1)}), bf16[8,2,64,256]{3,2,1,0:T(8,128)(2,1)}, u32[]{:S(2)}, u32[]{:S(2)}) async-start(bf16[8,2,64,256]{3,2,1,0:T(8,128)(2,1)} %copy.256), calls=%async_computation.8 | async-start | bytes 1048576 | tf_op jit(solution)/shard_map/all_to_all | solution.py:126
  256.3 169.6 %copy-start.1 = (bf16[1,1,8,64,4,256]{5,4,3,2,1,0:T(4,128)(2,1)S(1)}, bf16[1,1,8,64,4,256]{5,4,3,2,1,0:T(4,128)(2,1)}, u32[]{:S(2)}) copy-start(bf16[1,1,8,64,4,256]{5,4,3,2,1,0:T(4,128)(2,1)} %param.10) | copy-start | bytes 3145732
  (5 other events, 6.2 us)
Sparse Core Ops, SparseCore 0:
  11.2 91.3 all-gather.1
  181.4 15.5 reduce-scatter.3
  199.6 16.2 reduce-scatter.7
  219.6 204.6 reduce-scatter.5

commit v2 on v1

--- a/solution.py
+++ b/solution.py
@@ -44,6 +44,13 @@
     dk_own = jnp.einsum("bkgru,brkgd->bukd", ds_own, queries, preferred_element_type=f32) * scale
     dv_own = jnp.einsum("bkgru,brkgd->bukd", w_own, cotangent, preferred_element_type=f32)
     return output, dquery, dk_sh, dv_sh, dk_own, dv_own
+
+
+def scatter_sum(x, axis_name, dim):
+    n = lax.axis_size(axis_name)
+    got = lax.all_to_all(x, axis_name, split_axis=dim, concat_axis=dim, tiled=True)
+    shape = x.shape[:dim] + (n, x.shape[dim] // n) + x.shape[dim + 1 :]
+    return jnp.sum(got.reshape(shape), axis=dim)
 
 
 def body(prompt_q, prompt_kv, prompt_grad, resp_q, resp_kv, resp_grad, resp_prompt):
@@ -112,12 +119,12 @@
     dq = dq.astype(jnp.bfloat16).reshape(peers + 1, resp_len, kv_heads, local_width)
 
     prompt_part = jnp.stack([dk_sh, dv_sh]).reshape(2, full_len, kv_width)
-    head_sum = lax.psum_scatter(prompt_part, "head", scatter_dimension=2, tiled=True)
-    block_sum = lax.psum_scatter(head_sum, "prompt", scatter_dimension=1, tiled=True)
+    head_sum = scatter_sum(prompt_part, "head", 2)
+    block_sum = scatter_sum(head_sum, "prompt", 1)
     own_part = jnp.stack([dk_own[:peers], dv_own[:peers]], axis=1).reshape(
         peers, 2, resp_len, kv_width
     )
-    own_sum = lax.psum_scatter(own_part, "head", scatter_dimension=3, tiled=True)
+    own_sum = scatter_sum(own_part, "head", 3)
     prompt_dkv = block_sum.astype(jnp.bfloat16)[:, None]
     back_kv = own_sum.astype(jnp.bfloat16)
     ret_out, ret_dq, ret_kv = (

time: 440 us -> 377 us (0.86)
  waiting for transfers between devices: 248 us -> 114 us
  local copies, waits for them, and re-layouts: 60 us -> 79.2 us
  other arithmetic: 21.2 us -> 38.5 us
  blocking collectives: 0 us -> 17 us
  matrix products: 61.5 us -> 71.9 us
  starting transfers between devices: 27.4 us -> 36.2 us
    reduce_scatter x3 -> x0, waiting for transfers between devices: 162 us -> none  [the longest x1 161 us: body(): lax.psum_scatter(head_sum, 'prompt', scatter_dimension=1, tiled=True)]
    all_to_all x0 -> x1, waiting for transfers between devices: none -> 38.4 us  [scatter_sum(): lax.all_to_all(x, axis_name, split_axis=dim, concat_axis=dim, tiled=True)]
    all_to_all x0 -> x2, blocking collectives: none -> 17 us  [scatter_sum(): lax.all_to_all(x, axis_name, split_axis=dim, concat_axis=dim, tiled=True)]
    unnamed x64 -> x66, local copies, waits for them, and re-layouts: 24.6 us -> 34.8 us
    all_to_all x0 -> x1, other arithmetic: none -> 9.69 us  [scatter_sum(): lax.all_to_all(x, axis_name, split_axis=dim, concat_axis=dim, tiled=True)]
    reduce_sum x0 -> x3, other arithmetic: none -> 9.33 us  [scatter_sum(): return jnp.sum(got.reshape(shape), axis=dim)]
    all_to_all x1, waiting for transfers between devices: 13.5 us -> 6.01 us  [body(): lax.all_to_all(out[:peers], 'resp', split_axis=0, concat_axis=0, tiled=True)]
    all_to_all x0 -> x1, starting transfers between devices: none -> 7 us  [scatter_sum(): lax.all_to_all(x, axis_name, split_axis=dim, concat_axis=dim, tiled=True)]
  transfers between devices with their start and end apart: 10 -> 8, of which waited for: 9 -> 7; matrix products, arithmetic and copies ran while one was open for 13% -> 14% of each run, Pallas kernels for 0% -> 0%
where the time goes in v2:
time: 377 us; the launch traced here: 372 us
  waiting for transfers between devices  114 us (30%)
  local copies, waits for them, and re-layouts  79.2 us (21%)
  matrix products  71.9 us (19%)
  other arithmetic  38.5 us (10%)
  starting transfers between devices  36.2 us (10%)
  blocking collectives  17 us (5%)
  between operations  14.9 us (4%)
    all_to_all x1, waiting for transfers between devices, scatter_sum(): lax.all_to_all(x, axis_name, split_axis=dim, concat_axis=dim, tiled=True)  38.4 us
    unnamed x66, local copies, waits for them, and re-layouts  34.8 us
    all_gather x1, waiting for transfers between devices, body(): gathered = lax.all_gather(prompt_kv, 'prompt', axis=2, tiled=True)  19.2 us
    all_to_all x2, blocking collectives, scatter_sum(): lax.all_to_all(x, axis_name, split_axis=dim, concat_axis=dim, tiled=True)  17 us
    dot_general x1, matrix products, attend_blocks(): jnp.einsum('brkgd,nkd->bkgrn', cotangent, values_in, preferred_element_ty...  13.7 us
    all_to_all x1, waiting for transfers between devices, body(): lax.all_to_all(send_grad, 'resp', split_axis=0, concat_axis=0, tiled=True)  13.5 us
    dot_general x1, matrix products, attend_blocks(): jnp.einsum('bkgrn,nkd->brkgd', w_sh, values_in, preferred_element_type=f32)  12.9 us
    all_to_all x1, waiting for transfers between devices, body(): lax.all_to_all(send_q, 'resp', split_axis=0, concat_axis=0, tiled=True)  12.9 us
  transfers between devices with their start and end apart: 8, of which 7 were waited for; matrix products, arithmetic and copies ran while one was open for 14% of the time, Pallas kernels for 0%

profile of v2, /device:TPU:32, one launch (start us, length us, event | category | flops | bytes accessed | tf_op | source)
XLA Modules:
  0.0 371.6 jit_solution(10454590647678968120)
XLA Ops:
  11.9 5.4 %all-to-all-start = ((bf16[8,64,4,256]{3,2,1,0:T(4,128)(2,1)}), bf16[8,64,4,256]{3,2,1,0:T(4,128)(2,1)S(1)}, u32[]{:S(2)}, u32[]{:S(2)}) async-start(bf16[8,64,4,256]{3,2,1,0:T(4,128)(2,1)} %copy.208), calls=%async_computation | async-start | bytes 2097152 | tf_op jit(solution)/shard_map/all_to_all | solution.py:82
  19.4 12.9 %all-to-all-done = bf16[8,64,4,256]{3,2,1,0:T(4,128)(2,1)S(1)} async-done(((bf16[8,64,4,256]{3,2,1,0:T(4,128)(2,1)}), bf16[8,64,4,256]{3,2,1,0:T(4,128)(2,1)S(1)}, u32[]{:S(2)}, u32[]{:S(2)}) %all-to-all-start) | async-done | bytes 1048608 | tf_op jit(solution)/shard_map/all_to_all | solution.py:82
  32.3 4.2 %all-to-all-start.1 = ((bf16[8,2,64,512]{3,2,1,0:T(8,128)(2,1)}), bf16[8,2,64,512]{3,2,1,0:T(8,128)(2,1)S(1)}, u32[]{:S(2)}, u32[]{:S(2)}) async-start(bf16[8,2,64,512]{3,2,1,0:T(8,128)(2,1)} %copy.216), calls=%async_computation.1 | async-start | bytes 2097152 | tf_op jit(solution)/shard_map/all_to_all | solution.py:83
  38.8 11.9 %all-to-all-done.1 = bf16[8,2,64,512]{3,2,1,0:T(8,128)(2,1)S(1)} async-done(((bf16[8,2,64,512]{3,2,1,0:T(8,128)(2,1)}), bf16[8,2,64,512]{3,2,1,0:T(8,128)(2,1)S(1)}, u32[]{:S(2)}, u32[]{:S(2)}) %all-to-all-start.1) | async-done | bytes 1048608 | tf_op jit(solution)/shard_map/all_to_all | solution.py:83
  50.7 4.4 %all-to-all-start.2 = ((bf16[8,64,4,256]{3,2,1,0:T(4,128)(2,1)}), bf16[8,64,4,256]{3,2,1,0:T(4,128)(2,1)}, u32[]{:S(2)}, u32[]{:S(2)}) async-start(bf16[8,64,4,256]{3,2,1,0:T(4,128)(2,1)} %copy.234), calls=%async_computation.2 | async-start | bytes 2097152 | tf_op jit(solution)/shard_map/all_to_all | solution.py:84
  59.6 13.5 %all-to-all-done.2 = bf16[8,64,4,256]{3,2,1,0:T(4,128)(2,1)} async-done(((bf16[8,64,4,256]{3,2,1,0:T(4,128)(2,1)}), bf16[8,64,4,256]{3,2,1,0:T(4,128)(2,1)}, u32[]{:S(2)}, u32[]{:S(2)}) %all-to-all-start.2) | async-done | bytes 1048608 | tf_op jit(solution)/shard_map/all_to_all | solution.py:84
  83.5 19.2 %all-gather.2.cloned.1.call-done = bf16[2,1,1024,512]{3,0,1,2:T(2,128)(2,1)} async-done(((bf16[2,1,64,512]{3,0,1,2:T(2,128)(2,1)}), bf16[2,1,1024,512]{3,0,1,2:T(2,128)(2,1)}) %all-gather.2.cloned.1.call-update) | async-done | bytes 2097168 | tf_op jit(solution)/shard_map/all_gather | solution.py:66
  102.7 7.0 %fusion.60 = (bf16[1,1,1024,512]{3,0,1,2:T(2,128)(2,1)}, bf16[1,1,1024,512]{3,0,1,2:T(2,128)(2,1)}) fusion(bf16[2,1,1024,512]{3,0,1,2:T(2,128)(2,1)} %all-gather.2.cloned.1.call-done), kind=kLoop, calls=%fused_computation.87 | loop fusion | bytes 4194304 | tf_op jit(solution)/shard_map/slice | solution.py:68
  109.7 5.8 %copy.333 = bf16[1,1,1024,512]{2,3,1,0:T(8,128)(2,1)} copy(bf16[1,1,1024,512]{3,0,1,2:T(2,128)(2,1)} %get-tuple-element.37) | data formatting | bytes 2097152
  115.5 5.6 %bitcast_reduce_fusion = (f32[9,4,2,64]{3,2,0,1:T(2,128)S(1)}, f32[4,9,64,2,1024]{4,2,3,1,0:T(8,128)S(1)}) fusion(pred[9,64,1024]{2,1,0:T(8,128)(4,1)} %concatenate.17, bf16[1024,4,128,1,1]{0,2,4,3,1:T(8,128)(2,1)} %bitcast.165, bf16[9,64,4,2,128]{4,3,2,1,0:T(2,128)(2,1)} %reshape.136), kind=kOutput, calls=%fused_computation.5 | convolution fusion | flops 1222110720 | bytes 21710848 | tf_op jit(solution)/shard_map/brkgd,nkd->bkgrn/dot_general | solution.py:14
  121.2 5.4 %fusion.3 = f32[9,4,2,64]{3,2,0,1:T(2,128)S(1)} fusion(f32[4,9,64,2,1024]{4,2,3,1,0:T(8,128)S(1)} %get-tuple-element.43, f32[9,4,2,64]{3,2,0,1:T(2,128)S(1)} %copy.221, pred[9,64,1024]{2,1,0:T(8,128)(4,1)S(1)} %copy-done.13), kind=kLoop, calls=%fused_computation.7 | loop fusion | flops 18869760 | bytes 19501056 | tf_op jit(solution)/shard_map/reduce_sum | solution.py:21
  132.5 5.8 %copy.335 = bf16[1,1,1024,512]{2,3,1,0:T(8,128)(2,1)} copy(bf16[1,1,1024,512]{3,0,1,2:T(2,128)(2,1)} %get-tuple-element.36) | data formatting | bytes 2097152
  138.3 12.9 %multiply_reduce_fusion = (f32[9,4,2,64]{3,2,0,1:T(2,128)S(1)}, bf16[9,64,4,2,128]{4,1,3,0,2:T(8,128)(2,1)}) fusion(f32[9,4,2,64,128]{4,2,3,1,0:T(2,128)} %copy_convert_fusion, f32[9,4,128,2,64]{2,4,3,0,1:T(8,128)} %fusion.19, bf16[1024,4,128,1,1]{0,2,4,3,1:T(8,128)(2,1)} %bitcast.168, f32[4,9,64,2,1024]{4,2,3,1,0:T(8,128)} %copy-done.2, ...), kind=kOutput, calls=%fused_computation.21 | convolution fusion | flops 1229778432 | bytes 26447872 | tf_op jit(solution)/shard_map/bkgrn,nkd->brkgd/dot_general | solution.py:30
  152.7 13.7 %fusion.1 = bf16[9,4,2,64,1024]{4,3,2,0,1:T(8,128)(2,1)} fusion(f32[4,9,64,2,1024]{4,2,3,1,0:T(8,128)} %copy-done.2, f32[9,4,2,64]{3,2,0,1:T(2,128)S(1)} %get-tuple-element.44, f32[9,4,2,64]{3,2,0,1:T(2,128)S(1)} %copy.225, pred[9,64,1024]{2,1,0:T(8,128)(4,1)S(1)} %copy-done.14, bf16[1024,4,128,1,1]{0,2,4,3,1:T(8,128)(2,1)S(1)} %bitcast.169, ...), kind=kOutput, calls=%fused_computation.2 | convolution fusion | flops 1236271104 | bytes 31166464 | tf_op jit(solution)/shard_map/brkgd,nkd->bkgrn/dot_general | solution.py:34
  166.4 10.8 %fusion.28 = f32[4,128,1024,1,1]{2,1,4,3,0:T(8,128)} fusion(bf16[9,64,4,2,128]{4,3,2,1,0:T(2,128)(2,1)S(1)} %copy-done.5, f32[4,9,64,2,1024]{4,2,3,1,0:T(8,128)} %copy-done.2, f32[9,4,2,64]{3,2,0,1:T(2,128)S(1)} %copy.225, pred[9,64,1024]{2,1,0:T(8,128)(4,1)S(1)} %copy-done.14), kind=kOutput, calls=%fused_computation.54 | convolution fusion | flops 1226833920 | bytes 22759424 | tf_op jit(solution)/shard_map/bkgrn,brkgd->nkd/dot_general | solution.py:43
  189.6 4.8 %copy.261 = f32[8,2,64,512]{2,0,1,3:T(8,128)} copy(f32[8,2,64,512]{3,2,0,1:T(8,128)} %pad_maximum_fusion.1) | data formatting | bytes 4194304 | tf_op jit(solution)/shard_map/stack | solution.py:124
  194.4 5.3 %reshape.142 = f32[2,1,262144]{2,1,0:T(1,128)} reshape(f32[512,2,8,64]{3,2,1,0:T(8,128)} %bitcast.160) | data formatting | bytes 4194304
  199.7 8.6 %all_to_all.45 = f32[2,1,262144]{2,1,0:T(1,128)} all-to-all(f32[2,1,262144]{2,1,0:T(1,128)} %reshape.142), channel_id=1, replica_groups=mesh['prompt'=16,'resp'=8,'head'=2] {'head'}, dimensions={0} | all-to-all | bytes 4194304 | tf_op jit(solution)/shard_map/all_to_all | solution.py:51
  208.8 9.7 %reduce.2 = f32[2,262144]{1,0:T(2,128)} reduce(f32[2,1,262144]{2,1,0:T(1,128)} %all_to_all.45, f32[]{:T(128)} %broadcast.42), dimensions={1}, to_apply=%all_to_all.34.reduce_sub_computation | reduce | bytes 4194308 | tf_op jit(solution)/shard_map/all_to_all | solution.py:51
  218.5 5.8 %reshape.143 = f32[512,2,8,64]{3,2,1,0:T(8,128)} reshape(f32[2,262144]{1,0:T(2,128)} %reduce.2) | data formatting | bytes 4194304
  229.2 5.4 %bitcast_multiply_fusion = f32[4,128,1024]{2,1,0:T(8,128)S(1)} fusion(bf16[9,4,2,64,1024]{4,3,2,0,1:T(8,128)(2,1)} %fusion.1, bf16[9,64,4,2,128]{4,3,2,1,0:T(2,128)(2,1)S(1)} %copy-done.7), kind=kOutput, calls=%fused_computation.25 | convolution fusion | flops 1208483840 | bytes 12713984 | tf_op jit(solution)/shard_map/bkgrn,brkgd->nkd/dot_general | solution.py:42
  239.0 4.0 %pad_maximum_fusion = f32[2,1024,512]{1,0,2:T(2,128)S(1)} fusion(f32[1,1024,512]{1,0,2:T(1,128)S(1)} %copy.248, f32[1,1024,512]{1,0,2:T(1,128)S(1)} %copy.247), kind=kLoop, calls=%fused_computation.11 | loop fusion | flops 1048576 | bytes 8388608 | tf_op jit(solution)/shard_map/stack | solution.py:121
  243.0 8.4 %all_to_all.46 = f32[2,1024,512]{1,0,2:T(2,128)} all-to-all(f32[2,1024,512]{1,0,2:T(2,128)S(1)} %pad_maximum_fusion), channel_id=1, replica_groups=mesh['prompt'=16,'resp'=8,'head'=2] {'head'}, dimensions={2} | all-to-all | bytes 8388608 | tf_op jit(solution)/shard_map/all_to_all | solution.py:51
  251.4 4.9 %all-to-all-start.8 = ((bf16[8,2,64,256]{3,2,1,0:T(8,128)(2,1)}), bf16[8,2,64,256]{3,2,1,0:T(8,128)(2,1)}, u32[]{:S(2)}, u32[]{:S(2)}) async-start(bf16[8,2,64,256]{3,2,1,0:T(8,128)(2,1)} %copy.263), calls=%async_computation.8 | async-start | bytes 1048576 | tf_op jit(solution)/shard_map/all_to_all | solution.py:133
  256.3 6.3 %fusion.7 = bf16[9,64,4,2,128]{4,1,3,0,2:T(8,128)(2,1)S(1)} fusion(f32[9,4,128,2,64]{2,4,3,0,1:T(8,128)S(1)} %copy-done.8, bf16[9,4,2,64,1024]{4,3,2,0,1:T(8,128)(2,1)} %fusion.1, bf16[1024,4,128,1,1]{0,2,4,3,1:T(8,128)(2,1)S(1)} %bitcast.166), kind=kOutput, calls=%fused_computation.14 | convolution fusion | flops 1209729024 | bytes 14024704 | tf_op jit(solution)/shard_map/bkgrn,nkd->brkgd/dot_general | solution.py:39
  266.4 5.7 %all-to-all-start.6 = ((bf16[8,64,4,256]{3,2,1,0:T(4,128)(2,1)}), bf16[8,64,4,256]{3,2,1,0:T(4,128)(2,1)S(1)}, u32[]{:S(2)}, u32[]{:S(2)}) async-start(bf16[8,64,4,256]{3,2,1,0:T(4,128)(2,1)} %reshape.141), calls=%async_computation.6 | async-start | bytes 2097152 | tf_op jit(solution)/shard_map/all_to_all | solution.py:132
  274.7 11.9 %all-to-all-done.6 = bf16[8,64,4,256]{3,2,1,0:T(4,128)(2,1)S(1)} async-done(((bf16[8,64,4,256]{3,2,1,0:T(4,128)(2,1)}), bf16[8,64,4,256]{3,2,1,0:T(4,128)(2,1)S(1)}, u32[]{:S(2)}, u32[]{:S(2)}) %all-to-all-start.6) | async-done | bytes 1048608 | tf_op jit(solution)/shard_map/all_to_all | solution.py:132
  286.6 4.5 %all-to-all-start.5 = ((bf16[8,64,4,256]{3,2,1,0:T(4,128)(2,1)}), bf16[8,64,4,256]{3,2,1,0:T(4,128)(2,1)}, u32[]{:S(2)}, u32[]{:S(2)}) async-start(bf16[8,64,4,256]{3,2,1,0:T(4,128)(2,1)} %reshape.140), calls=%async_computation.5 | async-start | bytes 2097152 | tf_op jit(solution)/shard_map/all_to_all | solution.py:131
  291.1 5.3 %reduce_sum.47 = f32[2,1024,256]{1,0,2:T(2,128)S(1)} reduce(f32[2,1024,2,256]{1,0,3,2:T(2,128)} %bitcast.161, f32[]{:T(128)} %constant.8.clone.1), dimensions={2}, to_apply=%region_4.5 | reduce | flops 524288 | bytes 6291460 | tf_op jit(solution)/shard_map/reduce_sum | solution.py:53
  299.7 6.0 %all-to-all-done.5 = bf16[8,64,4,256]{3,2,1,0:T(4,128)(2,1)} async-done(((bf16[8,64,4,256]{3,2,1,0:T(4,128)(2,1)}), bf16[8,64,4,256]{3,2,1,0:T(4,128)(2,1)}, u32[]{:S(2)}, u32[]{:S(2)}) %all-to-all-start.5) | async-done | bytes 1048608 | tf_op jit(solution)/shard_map/all_to_all | solution.py:131
  305.7 7.0 %all-to-all-start.4 = ((f32[2,1024,256]{2,0,1:T(2,128)}), f32[2,1024,256]{2,0,1:T(2,128)S(1)}, u32[]{:S(2)}, u32[]{:S(2)}) async-start(f32[2,1024,256]{2,0,1:T(2,128)} %copy.250), calls=%async_computation.4 | async-start | bytes 4194304 | tf_op jit(solution)/shard_map/all_to_all | solution.py:51
  324.6 38.4 %all-to-all-done.4 = f32[2,1024,256]{2,0,1:T(2,128)S(1)} async-done(((f32[2,1024,256]{2,0,1:T(2,128)}), f32[2,1024,256]{2,0,1:T(2,128)S(1)}, u32[]{:S(2)}, u32[]{:S(2)}) %all-to-all-start.4) | async-done | bytes 2097184 | tf_op jit(solution)/shard_map/all_to_all | solution.py:51
  (125 shorter events, 76.0 us)
Async XLA Ops:
  7.2 1.9 copy-start
  7.2 95.5 %all-gather.2.cloned.1.call-start = ((), (), s32[]{:S(2)}) async-start(), calls=%async_computation.9 | async-start | bytes 2228224 | tf_op jit(solution)/shard_map/all_gather | solution.py:66
  10.5 6.8 %copy-start.20 = (bf16[2,1,1,8,64,512]{5,4,3,2,1,0:T(8,128)(2,1)S(1)}, bf16[2,1,1,8,64,512]{5,4,3,2,1,0:T(8,128)(2,1)}, u32[]{:S(2)}) copy-start(bf16[2,1,1,8,64,512]{5,4,3,2,1,0:T(8,128)(2,1)} %param.11) | copy-start | bytes 3145732
  10.5 6.8 %copy-start.25 = (s32[1,1,8]{2,1,0:T(1,128)S(1)}, s32[1,1,8]{2,1,0:T(1,128)}, u32[]{:S(2)}) copy-start(s32[1,1,8]{2,1,0:T(1,128)} %param.13) | copy-start | bytes 100
  11.9 20.4 %all-to-all-start = ((bf16[8,64,4,256]{3,2,1,0:T(4,128)(2,1)}), bf16[8,64,4,256]{3,2,1,0:T(4,128)(2,1)S(1)}, u32[]{:S(2)}, u32[]{:S(2)}) async-start(bf16[8,64,4,256]{3,2,1,0:T(4,128)(2,1)} %copy.208), calls=%async_computation | async-start | bytes 2097152 | tf_op jit(solution)/shard_map/all_to_all | solution.py:82
  18.1 18.5 %copy-start.21 = (bf16[1,1,8,64,4,256]{5,4,3,2,1,0:T(4,128)(2,1)S(1)}, bf16[1,1,8,64,4,256]{5,4,3,2,1,0:T(4,128)(2,1)}, u32[]{:S(2)}) copy-start(bf16[1,1,8,64,4,256]{5,4,3,2,1,0:T(4,128)(2,1)} %param.12) | copy-start | bytes 3145732
  32.3 18.4 %all-to-all-start.1 = ((bf16[8,2,64,512]{3,2,1,0:T(8,128)(2,1)}), bf16[8,2,64,512]{3,2,1,0:T(8,128)(2,1)S(1)}, u32[]{:S(2)}, u32[]{:S(2)}) async-start(bf16[8,2,64,512]{3,2,1,0:T(8,128)(2,1)} %copy.216), calls=%async_computation.1 | async-start | bytes 2097152 | tf_op jit(solution)/shard_map/all_to_all | solution.py:83
  37.4 19.6 %copy-start.22 = (bf16[1,64,4,256]{3,2,1,0:T(4,128)(2,1)S(1)}, bf16[1,64,4,256]{3,2,1,0:T(4,128)(2,1)}, u32[]{:S(2)}) copy-start(bf16[1,64,4,256]{3,2,1,0:T(4,128)(2,1)} %param.7) | copy-start | bytes 393220
  50.7 22.4 %all-to-all-start.2 = ((bf16[8,64,4,256]{3,2,1,0:T(4,128)(2,1)}), bf16[8,64,4,256]{3,2,1,0:T(4,128)(2,1)}, u32[]{:S(2)}, u32[]{:S(2)}) async-start(bf16[8,64,4,256]{3,2,1,0:T(4,128)(2,1)} %copy.234), calls=%async_computation.2 | async-start | bytes 2097152 | tf_op jit(solution)/shard_map/all_to_all | solution.py:84
  59.1 14.0 %copy-start.23 = (bf16[1,64,4,256]{3,2,1,0:T(4,128)(2,1)S(1)}, bf16[1,64,4,256]{3,2,1,0:T(4,128)(2,1)}, u32[]{:S(2)}) copy-start(bf16[1,64,4,256]{3,2,1,0:T(4,128)(2,1)} %param.9) | copy-start | bytes 393220
  79.0 3.2 copy-start.3
  79.5 2.7 copy-start.15
  79.5 2.7 copy-start.6
  79.5 2.7 copy-start.24
  115.5 5.7 %copy-start.13 = (pred[9,64,1024]{2,1,0:T(8,128)(4,1)S(1)}, pred[9,64,1024]{2,1,0:T(8,128)(4,1)}, u32[]{:S(2)}) copy-start(pred[9,64,1024]{2,1,0:T(8,128)(4,1)} %concatenate.17) | copy-start | bytes 1769476
  121.1 6.5 %copy-start.2 = (f32[4,9,64,2,1024]{4,2,3,1,0:T(8,128)}, f32[4,9,64,2,1024]{4,2,3,1,0:T(8,128)S(1)}, u32[]{:S(2)}) copy-start(f32[4,9,64,2,1024]{4,2,3,1,0:T(8,128)S(1)} %get-tuple-element.43) | copy-start | bytes 56623108
  138.3 13.0 %copy-start.5 = (bf16[9,64,4,2,128]{4,3,2,1,0:T(2,128)(2,1)S(1)}, bf16[9,64,4,2,128]{4,3,2,1,0:T(2,128)(2,1)}, u32[]{:S(2)}) copy-start(bf16[9,64,4,2,128]{4,3,2,1,0:T(2,128)(2,1)} %copy-done.3) | copy-start | bytes 3538948
  151.3 1.4 copy-start.19
  166.4 10.8 %copy-start.7 = (bf16[9,64,4,2,128]{4,3,2,1,0:T(2,128)(2,1)S(1)}, bf16[9,64,4,2,128]{4,3,2,1,0:T(2,128)(2,1)}, u32[]{:S(2)}) copy-start(bf16[9,64,4,2,128]{4,3,2,1,0:T(2,128)(2,1)} %reshape.136) | copy-start | bytes 3538948
  178.3 2.0 slice-start.1
  185.3 1.4 copy-start.11
  234.6 2.2 copy-start.17
  243.0 13.3 %copy-start.8 = (f32[9,4,128,2,64]{2,4,3,0,1:T(8,128)S(1)}, f32[9,4,128,2,64]{2,4,3,0,1:T(8,128)}, u32[]{:S(2)}) copy-start(f32[9,4,128,2,64]{2,4,3,0,1:T(8,128)} %fusion.17) | copy-start | bytes 7077892
  243.0 13.3 %copy-start.12 = (bf16[1,1,1024,512]{2,3,1,0:T(8,128)(2,1)S(1)}, bf16[1,1,1024,512]{2,3,1,0:T(8,128)(2,1)}, u32[]{:S(2)}) copy-start(bf16[1,1,1024,512]{2,3,1,0:T(8,128)(2,1)} %copy.333) | copy-start | bytes 3145732
  251.4 15.0 %all-to-all-start.8 = ((bf16[8,2,64,256]{3,2,1,0:T(8,128)(2,1)}), bf16[8,2,64,256]{3,2,1,0:T(8,128)(2,1)}, u32[]{:S(2)}, u32[]{:S(2)}) async-start(bf16[8,2,64,256]{3,2,1,0:T(8,128)(2,1)} %copy.263), calls=%async_computation.8 | async-start | bytes 1048576 | tf_op jit(solution)/shard_map/all_to_all | solution.py:133
  264.9 7.2 %copy-start.18 = (bf16[9,64,4,2,128]{4,1,3,0,2:T(8,128)(2,1)S(1)}, bf16[9,64,4,2,128]{4,1,3,0,2:T(8,128)(2,1)}, u32[]{:S(2)}) copy-start(bf16[9,64,4,2,128]{4,1,3,0,2:T(8,128)(2,1)} %get-tuple-element.45) | copy-start | bytes 3538948
  266.4 20.2 %all-to-all-start.6 = ((bf16[8,64,4,256]{3,2,1,0:T(4,128)(2,1)}), bf16[8,64,4,256]{3,2,1,0:T(4,128)(2,1)S(1)}, u32[]{:S(2)}, u32[]{:S(2)}) async-start(bf16[8,64,4,256]{3,2,1,0:T(4,128)(2,1)} %reshape.141), calls=%async_computation.6 | async-start | bytes 2097152 | tf_op jit(solution)/shard_map/all_to_all | solution.py:132
  286.6 9.8 %copy-start.10 = (bf16[8,64,4,256]{3,2,1,0:T(4,128)(2,1)}, bf16[8,64,4,256]{3,2,1,0:T(4,128)(2,1)S(1)}, u32[]{:S(2)}) copy-start(bf16[8,64,4,256]{3,2,1,0:T(4,128)(2,1)S(1)} %all-to-all-done.6) | copy-start | bytes 3145732
  286.6 19.1 %all-to-all-start.5 = ((bf16[8,64,4,256]{3,2,1,0:T(4,128)(2,1)}), bf16[8,64,4,256]{3,2,1,0:T(4,128)(2,1)}, u32[]{:S(2)}, u32[]{:S(2)}) async-start(bf16[8,64,4,256]{3,2,1,0:T(4,128)(2,1)} %reshape.140), calls=%async_computation.5 | async-start | bytes 2097152 | tf_op jit(solution)/shard_map/all_to_all | solution.py:131
  299.7 13.9 %slice-start = ((bf16[9,64,4,2,128]{4,1,3,0,2:T(8,128)(2,1)}), bf16[1,64,4,2,128]{4,1,3,0,2:T(8,128)(2,1)S(1)}, s32[]{:S(2)}) async-start(bf16[9,64,4,2,128]{4,1,3,0,2:T(8,128)(2,1)} %copy-done.9), calls=%async_computation.10 | async-start | bytes 262144 | tf_op jit(solution)/shard_map/slice | solution.py:145
  305.7 57.2 %all-to-all-start.4 = ((f32[2,1024,256]{2,0,1:T(2,128)}), f32[2,1024,256]{2,0,1:T(2,128)S(1)}, u32[]{:S(2)}, u32[]{:S(2)}) async-start(f32[2,1024,256]{2,0,1:T(2,128)} %copy.250), calls=%async_computation.4 | async-start | bytes 4194304 | tf_op jit(solution)/shard_map/all_to_all | solution.py:51
  321.2 43.3 %copy-start.1 = (bf16[1,1,8,64,4,256]{5,4,3,2,1,0:T(4,128)(2,1)S(1)}, bf16[1,1,8,64,4,256]{5,4,3,2,1,0:T(4,128)(2,1)}, u32[]{:S(2)}) copy-start(bf16[1,1,8,64,4,256]{5,4,3,2,1,0:T(4,128)(2,1)} %param.10) | copy-start | bytes 3145732
  (4 other events, 4.7 us)
Sparse Core Ops, SparseCore 0:
  11.2 91.4 all-gather.1

commit v3 on v2

--- a/solution.py
+++ b/solution.py
@@ -63,30 +63,34 @@
     resp_len = resp_q.shape[3]
     peers = lax.axis_size("resp")
     kv_width = kv_heads * head_size
+    q_width = kv_heads * local_width
     gathered = lax.all_gather(prompt_kv, "prompt", axis=2, tiled=True)
     prompt_keys = gathered[0, 0].reshape(full_len, kv_heads, head_size)
     prompt_values = gathered[1, 0].reshape(full_len, kv_heads, head_size)
 
     order = resp_prompt[0, 0]
     picker = (jnp.arange(peers)[:, None] == order[None, :]).astype(jnp.bfloat16)
-    send_q = jnp.einsum(
-        "dj,jrkh->drkh", picker, resp_q[0, 0], preferred_element_type=jnp.float32
+    stacked = jnp.concatenate(
+        [
+            resp_q[0, 0].reshape(peers, resp_len, q_width),
+            jnp.moveaxis(resp_kv[:, 0, 0], 0, 2).reshape(peers, resp_len, 2 * kv_width),
+            resp_grad[0, 0].reshape(peers, resp_len, q_width),
+        ],
+        axis=-1,
+    )
+    send = jnp.einsum(
+        "dj,jrh->drh", picker, stacked, preferred_element_type=jnp.float32
     ).astype(jnp.bfloat16)
-    send_kv = jnp.einsum(
-        "dj,cjrh->dcrh", picker, resp_kv[:, 0, 0], preferred_element_type=jnp.float32
-    ).astype(jnp.bfloat16)
-    send_grad = jnp.einsum(
-        "dj,jrkh->drkh", picker, resp_grad[0, 0], preferred_element_type=jnp.float32
-    ).astype(jnp.bfloat16)
-    got_q, got_kv, got_grad = (
-        lax.all_to_all(send_q, "resp", split_axis=0, concat_axis=0, tiled=True),
-        lax.all_to_all(send_kv, "resp", split_axis=0, concat_axis=0, tiled=True),
-        lax.all_to_all(send_grad, "resp", split_axis=0, concat_axis=0, tiled=True),
+    got = lax.all_to_all(send, "resp", split_axis=0, concat_axis=0, tiled=True)
+    got_q = got[..., :q_width]
+    got_kv = jnp.moveaxis(
+        got[..., q_width : q_width + 2 * kv_width].reshape(peers, resp_len, 2, kv_width), 2, 1
     )
+    got_grad = got[..., q_width + 2 * kv_width :]
 
     q_shape = (peers + 1, resp_len, kv_heads, local_heads, head_size)
-    queries = jnp.concatenate([got_q, prompt_q], axis=0).reshape(q_shape)
-    cotangent = jnp.concatenate([got_grad, prompt_grad], axis=0).reshape(q_shape)
+    queries = jnp.concatenate([got_q, prompt_q[0].reshape(1, resp_len, q_width)], axis=0).reshape(q_shape)
+    cotangent = jnp.concatenate([got_grad, prompt_grad[0].reshape(1, resp_len, q_width)], axis=0).reshape(q_shape)
     own_kv = jnp.concatenate(
         [got_kv, jnp.zeros((1,) + got_kv.shape[1:], got_kv.dtype)], axis=0
     ).reshape(peers + 1, 2, resp_len, kv_heads, head_size)
@@ -127,20 +131,25 @@
     own_sum = scatter_sum(own_part, "head", 3)
     prompt_dkv = block_sum.astype(jnp.bfloat16)[:, None]
     back_kv = own_sum.astype(jnp.bfloat16)
-    ret_out, ret_dq, ret_kv = (
-        lax.all_to_all(out[:peers], "resp", split_axis=0, concat_axis=0, tiled=True),
-        lax.all_to_all(dq[:peers], "resp", split_axis=0, concat_axis=0, tiled=True),
-        lax.all_to_all(back_kv, "resp", split_axis=0, concat_axis=0, tiled=True),
+    back = jnp.concatenate(
+        [
+            out[:peers].reshape(peers, resp_len, q_width),
+            dq[:peers].reshape(peers, resp_len, q_width),
+            jnp.moveaxis(back_kv, 1, 2).reshape(peers, resp_len, kv_width),
+        ],
+        axis=-1,
     )
-    resp_out = jnp.einsum(
-        "dj,drkh->jrkh", picker, ret_out, preferred_element_type=jnp.float32
-    ).astype(jnp.bfloat16)[None, None]
-    resp_dq = jnp.einsum(
-        "dj,drkh->jrkh", picker, ret_dq, preferred_element_type=jnp.float32
-    ).astype(jnp.bfloat16)[None, None]
-    resp_dkv = jnp.einsum(
-        "dj,dcrh->cjrh", picker, ret_kv, preferred_element_type=jnp.float32
-    ).astype(jnp.bfloat16)[:, None, None]
+    ret = lax.all_to_all(back, "resp", split_axis=0, concat_axis=0, tiled=True)
+    mine = jnp.einsum(
+        "dj,drh->jrh", picker, ret, preferred_element_type=jnp.float32
+    ).astype(jnp.bfloat16)
+    resp_out = mine[..., :q_width].reshape(peers, resp_len, kv_heads, local_width)[None, None]
+    resp_dq = mine[..., q_width : 2 * q_width].reshape(
+        peers, resp_len, kv_heads, local_width
+    )[None, None]
+    resp_dkv = jnp.moveaxis(
+        mine[..., 2 * q_width :].reshape(peers, resp_len, 2, kv_width // 2), 2, 0
+    )[:, None, None]
     prompt_out = out[peers:]
     prompt_dq = dq[peers:]
     return (prompt_out, prompt_dq, prompt_dkv, resp_out, resp_dq, resp_dkv)

time: 377 us -> 374 us (level)
  matrix products: 71.9 us -> 45.4 us
  waiting for transfers between devices: 114 us -> 136 us
  local copies, waits for them, and re-layouts: 79.2 us -> 97.8 us
  blocking collectives: 17 us -> 0 us
  starting transfers between devices: 36.2 us -> 26.7 us
  other arithmetic: 38.5 us -> 46.9 us
    all_gather x1, waiting for transfers between devices: 19.2 us -> 41.9 us  [body(): gathered = lax.all_gather(prompt_kv, 'prompt', axis=2, tiled=True)]
    all_to_all x6 -> x2, starting transfers between devices: 29.1 us -> 10.1 us  [the longest x1 5.53 us: body(): got = lax.all_to_all(send, 'resp', split_axis=0, concat_axis=0, tiled=True)]
    all_to_all x2 -> x0, blocking collectives: 17 us -> none  [scatter_sum(): lax.all_to_all(x, axis_name, split_axis=dim, concat_axis=dim, tiled=True)]
    all_to_all x1 -> x3, starting transfers between devices: 7 us -> 16.4 us  [scatter_sum(): lax.all_to_all(x, axis_name, split_axis=dim, concat_axis=dim, tiled=True)]
    dot_general x1, matrix products: 12.9 us -> 3.76 us  [attend_blocks(): jnp.einsum('bkgrn,nkd->brkgd', w_sh, values_in, preferred_element_type=f32)]
    convert_element_type x0 -> x1, other arithmetic: none -> 8.77 us  [attend_blocks(): w_sh = p_sh.astype(jnp.bfloat16)]
    dot_general x1, matrix products: 10.8 us -> 3.06 us  [attend_blocks(): jnp.einsum('bkgrn,brkgd->nkd', w_sh, cotangent, preferred_element_type=f32)]
    concatenate x0 -> x6, local copies, waits for them, and re-layouts: none -> 7.16 us  [the longest x3 4.49 us: body(): jnp.concatenate([got_grad, prompt_grad[0].reshape(1, resp_len, q_width)],...]
  transfers between devices with their start and end apart: 8 -> 6, of which waited for: 7 -> 4; matrix products, arithmetic and copies ran while one was open for 14% -> 18% of each run, Pallas kernels for 0% -> 0%
where the time goes in v3:
time: 374 us; the launch traced here: 368 us
  waiting for transfers between devices  136 us (36%)
  local copies, waits for them, and re-layouts  97.8 us (26%)
  other arithmetic  46.9 us (13%)
  matrix products  45.4 us (12%)
  starting transfers between devices  26.7 us (7%)
  between operations  15.1 us (4%)
    all_gather x1, waiting for transfers between devices, body(): gathered = lax.all_gather(prompt_kv, 'prompt', axis=2, tiled=True)  41.9 us
    all_to_all x3, waiting for transfers between devices, scatter_sum(): lax.all_to_all(x, axis_name, split_axis=dim, concat_axis=dim, tiled=True)  40.7 us
    unnamed x75, local copies, waits for them, and re-layouts  38.4 us
    all_to_all x1, waiting for transfers between devices, body(): got = lax.all_to_all(send, 'resp', split_axis=0, concat_axis=0, tiled=True)  32.9 us
    all_to_all x1, waiting for transfers between devices, body(): ret = lax.all_to_all(back, 'resp', split_axis=0, concat_axis=0, tiled=True)  20.4 us
    all_to_all x3, starting transfers between devices, scatter_sum(): lax.all_to_all(x, axis_name, split_axis=dim, concat_axis=dim, tiled=True)  16.4 us
    dot_general x1, matrix products, attend_blocks(): jnp.einsum('brkgd,nkd->bkgrn', cotangent, values_in, preferred_element_ty...  13.8 us
    reduce_sum x3, other arithmetic, scatter_sum(): return jnp.sum(got.reshape(shape), axis=dim)  12.1 us
  transfers between devices with their start and end apart: 6, of which 4 were waited for; matrix products, arithmetic and copies ran while one was open for 18% of the time, Pallas kernels for 0%

profile of v3, /device:TPU:32, one launch (start us, length us, event | category | flops | bytes accessed | tf_op | source)
XLA Modules:
  0.0 367.7 jit_solution(12576376994250348696)
XLA Ops:
  13.8 3.4 copy.244
  17.2 5.5 %all-to-all-start = ((bf16[8,64,3072]{2,1,0:T(8,128)(2,1)}), bf16[8,64,3072]{2,1,0:T(8,128)(2,1)S(1)}, u32[]{:S(2)}, u32[]{:S(2)}) async-start(bf16[8,64,3072]{2,1,0:T(8,128)(2,1)} %copy.244), calls=%async_computation | async-start | bytes 6291456 | tf_op jit(solution)/shard_map/all_to_all | solution.py:84
  27.3 32.9 %all-to-all-done = bf16[8,64,3072]{2,1,0:T(8,128)(2,1)S(1)} async-done(((bf16[8,64,3072]{2,1,0:T(8,128)(2,1)}), bf16[8,64,3072]{2,1,0:T(8,128)(2,1)S(1)}, u32[]{:S(2)}, u32[]{:S(2)}) %all-to-all-start) | async-done | bytes 3145760 | tf_op jit(solution)/shard_map/all_to_all | solution.py:84
  72.6 41.9 %all-gather.2.cloned.1.call-done = bf16[2,1,1024,512]{3,0,1,2:T(2,128)(2,1)} async-done(((bf16[2,1,64,512]{3,0,1,2:T(2,128)(2,1)}), bf16[2,1,1024,512]{3,0,1,2:T(2,128)(2,1)}) %all-gather.2.cloned.1.call-update) | async-done | bytes 2097168 | tf_op jit(solution)/shard_map/all_gather | solution.py:67
  114.5 6.7 %fusion.53 = (bf16[1,1,1024,512]{3,0,1,2:T(2,128)(2,1)}, bf16[1,1,1024,512]{3,0,1,2:T(2,128)(2,1)}) fusion(bf16[2,1,1024,512]{3,0,1,2:T(2,128)(2,1)} %all-gather.2.cloned.1.call-done), kind=kLoop, calls=%fused_computation.85 | loop fusion | bytes 4194304 | tf_op jit(solution)/shard_map/slice | solution.py:69
  121.3 5.8 %copy.349 = bf16[1,1,1024,512]{2,3,1,0:T(8,128)(2,1)} copy(bf16[1,1,1024,512]{3,0,1,2:T(2,128)(2,1)} %get-tuple-element.48) | data formatting | bytes 2097152
  127.1 4.9 %bitcast_reduce_fusion = (f32[9,4,2,64]{3,2,0,1:T(2,128)S(1)}, f32[4,9,64,2,1024]{4,2,3,1,0:T(8,128)S(1)}) fusion(pred[9,64,1024]{2,1,0:T(8,128)(4,1)} %concatenate.33, bf16[9,64,4,2,128]{4,1,3,0,2:T(8,128)(2,1)} %copy-done.8, bf16[1024,4,128,1,1]{0,2,4,3,1:T(8,128)(2,1)} %bitcast.173), kind=kOutput, calls=%fused_computation.5 | convolution fusion | flops 1222110720 | bytes 21710848 | tf_op jit(solution)/shard_map/brkgd,nkd->bkgrn/dot_general | solution.py:14
  133.5 5.5 %fusion.3 = f32[9,4,2,64]{3,2,0,1:T(2,128)S(1)} fusion(f32[4,9,64,2,1024]{4,2,3,1,0:T(8,128)S(1)} %get-tuple-element.54, f32[9,4,2,64]{3,2,0,1:T(2,128)S(1)} %copy.256, pred[9,64,1024]{2,1,0:T(8,128)(4,1)S(1)} %copy-done.4), kind=kLoop, calls=%fused_computation.7 | loop fusion | flops 18869760 | bytes 19501056 | tf_op jit(solution)/shard_map/reduce_sum | solution.py:21
  140.3 5.8 %copy.351 = bf16[1,1,1024,512]{2,3,1,0:T(8,128)(2,1)} copy(bf16[1,1,1024,512]{3,0,1,2:T(2,128)(2,1)} %get-tuple-element.47) | data formatting | bytes 2097152
  148.6 8.8 %fusion.5 = bf16[9,4,2,64,1024]{4,3,2,0,1:T(8,128)(2,1)S(1)} fusion(f32[4,9,64,2,1024]{4,2,3,1,0:T(8,128)} %copy-done, f32[9,4,2,64]{3,2,0,1:T(2,128)S(1)} %copy-done.20, pred[9,64,1024]{2,1,0:T(8,128)(4,1)S(1)} %copy-done.5), kind=kLoop, calls=%fused_computation.10 | loop fusion | flops 18874368 | bytes 28919808 | tf_op jit(solution)/shard_map/convert_element_type | solution.py:27
  157.4 3.1 fusion.6
  160.4 3.8 %fusion.20 = (f32[9,4,2,64]{3,2,0,1:T(2,128)S(1)}, bf16[9,64,4,2,128]{4,1,3,0,2:T(8,128)(2,1)}) fusion(bf16[9,64,4,2,128]{4,1,3,0,2:T(8,128)(2,1)S(1)} %copy_dynamic-update-slice_fusion.2, f32[9,4,128,2,64]{2,4,3,0,1:T(8,128)S(1)} %fusion.29, bf16[9,4,2,64,1024]{4,3,2,0,1:T(8,128)(2,1)S(1)} %fusion.5, bf16[1024,4,128,1,1]{0,2,4,3,1:T(8,128)(2,1)S(1)} %bitcast.167), kind=kOutput, calls=%fused_computation.32 | convolution fusion | flops 1211493888 | bytes 15222784 | tf_op jit(solution)/shard_map/bkgrn,nkd->brkgd/dot_general | solution.py:30
  164.2 13.8 %fusion.1 = bf16[9,4,2,64,1024]{4,3,2,0,1:T(8,128)(2,1)} fusion(f32[4,9,64,2,1024]{4,2,3,1,0:T(8,128)} %copy-done, f32[9,4,2,64]{3,2,0,1:T(2,128)S(1)} %get-tuple-element.55, f32[9,4,2,64]{3,2,0,1:T(2,128)S(1)} %copy-done.20, pred[9,64,1024]{2,1,0:T(8,128)(4,1)S(1)} %copy-done.5, bf16[9,64,4,2,128]{4,1,3,0,2:T(8,128)(2,1)S(1)} %copy_dynamic-update-slice_fusion.2, ...), kind=kOutput, calls=%fused_computation.2 | convolution fusion | flops 1236271104 | bytes 31166464 | tf_op jit(solution)/shard_map/brkgd,nkd->bkgrn/dot_general | solution.py:34
  183.5 5.2 %copy.283 = f32[1,1024,512]{1,0,2:T(1,128)} copy(f32[1,1024,512]{1,2,0:T(8,128)} %bitcast.177) | data formatting | bytes 4194304 | tf_op jit(solution)/shard_map/stack | solution.py:125
  190.9 2.8 reshape.138
  195.4 2.7 stack.21
  198.1 5.8 %bitcast_multiply_fusion = f32[4,128,1024]{2,1,0:T(8,128)S(1)} fusion(bf16[9,4,2,64,1024]{4,3,2,0,1:T(8,128)(2,1)} %fusion.1, bf16[9,64,4,2,128]{4,1,3,0,2:T(8,128)(2,1)} %copy-done.8), kind=kOutput, calls=%fused_computation.39 | convolution fusion | flops 1208483840 | bytes 12713984 | tf_op jit(solution)/shard_map/bkgrn,brkgd->nkd/dot_general | solution.py:42
  207.5 3.5 copy.282
  214.8 3.8 %copy.292 = f32[8,2,64,512]{2,0,1,3:T(8,128)} copy(f32[8,2,64,512]{3,2,0,1:T(8,128)S(1)} %pad_maximum_fusion.2) | data formatting | bytes 4194304 | tf_op jit(solution)/shard_map/stack | solution.py:128
  218.5 5.2 %reshape.164 = f32[2,1,262144]{2,1,0:T(1,128)} reshape(f32[512,2,8,64]{3,2,1,0:T(8,128)} %bitcast.162) | data formatting | bytes 4194304
  223.8 4.0 %all-to-all-start.3 = ((f32[2,1,262144]{2,1,0:T(1,128)}), f32[2,1,262144]{2,1,0:T(1,128)S(1)}, u32[]{:S(2)}, u32[]{:S(2)}) async-start(f32[2,1,262144]{2,1,0:T(1,128)} %reshape.164), calls=%async_computation.3 | async-start | bytes 4194304 | tf_op jit(solution)/shard_map/all_to_all | solution.py:51
  227.7 8.0 %pad_maximum_fusion = f32[2,1024,512]{1,0,2:T(2,128)} fusion(f32[1,1024,512]{1,0,2:T(1,128)} %copy.283, f32[1,1024,512]{1,0,2:T(1,128)} %copy.282), kind=kLoop, calls=%fused_computation.17 | loop fusion | flops 1048576 | bytes 8388608 | tf_op jit(solution)/shard_map/stack | solution.py:125
  237.1 5.6 %all-to-all-start.1 = ((f32[2,1024,512]{1,0,2:T(2,128)}), f32[2,1024,512]{1,0,2:T(2,128)}, u32[]{:S(2)}, u32[]{:S(2)}) async-start(f32[2,1024,512]{1,0,2:T(2,128)} %pad_maximum_fusion), calls=%async_computation.1 | async-start | bytes 8388608 | tf_op jit(solution)/shard_map/all_to_all | solution.py:51
  243.2 8.1 %reduce.2 = f32[2,262144]{1,0:T(2,128)S(1)} reduce(f32[2,1,262144]{2,1,0:T(1,128)} %copy-done.2, f32[]{:T(128)} %broadcast.42), dimensions={1}, to_apply=%all_to_all.18.reduce_sub_computation | reduce | bytes 4194308 | tf_op jit(solution)/shard_map/all_to_all | solution.py:51
  251.4 4.3 %reshape.165 = f32[512,2,8,64]{3,2,1,0:T(8,128)} reshape(f32[2,262144]{1,0:T(2,128)S(1)} %reduce.2) | data formatting | bytes 4194304
  255.6 3.3 reduce_sum.49
  263.4 4.6 %all-to-all-start.4 = ((bf16[8,64,2560]{2,1,0:T(8,128)(2,1)}), bf16[8,64,2560]{2,1,0:T(8,128)(2,1)S(1)}, u32[]{:S(2)}, u32[]{:S(2)}) async-start(bf16[8,64,2560]{2,1,0:T(8,128)(2,1)} %pad_maximum_fusion.1), calls=%async_computation.4 | async-start | bytes 5242880 | tf_op jit(solution)/shard_map/all_to_all | solution.py:142
  268.0 6.6 %reduce_sum.47 = f32[2,1024,256]{1,0,2:T(2,128)} reduce(f32[2,1024,2,256]{1,0,3,2:T(2,128)} %bitcast.40, f32[]{:T(128)} %constant.8.clone.1), dimensions={2}, to_apply=%region_4.5 | reduce | flops 524288 | bytes 6291460 | tf_op jit(solution)/shard_map/reduce_sum | solution.py:53
  274.6 5.3 %copy.285 = f32[2,1024,256]{2,0,1:T(2,128)} copy(f32[2,1024,256]{1,0,2:T(2,128)} %reduce_sum.47) | data formatting | bytes 4194304 | tf_op jit(solution)/shard_map/reduce_sum | solution.py:53
  279.9 20.4 %all-to-all-done.4 = bf16[8,64,2560]{2,1,0:T(8,128)(2,1)S(1)} async-done(((bf16[8,64,2560]{2,1,0:T(8,128)(2,1)}), bf16[8,64,2560]{2,1,0:T(8,128)(2,1)S(1)}, u32[]{:S(2)}, u32[]{:S(2)}) %all-to-all-start.4) | async-done | bytes 2621472 | tf_op jit(solution)/shard_map/all_to_all | solution.py:142
  300.3 6.7 %all-to-all-start.2 = ((f32[2,1024,256]{2,0,1:T(2,128)}), f32[2,1024,256]{2,0,1:T(2,128)}, u32[]{:S(2)}, u32[]{:S(2)}) async-start(f32[2,1024,256]{2,0,1:T(2,128)} %copy.285), calls=%async_computation.2 | async-start | bytes 4194304 | tf_op jit(solution)/shard_map/all_to_all | solution.py:51
  316.8 40.7 %all-to-all-done.2 = f32[2,1024,256]{2,0,1:T(2,128)} async-done(((f32[2,1024,256]{2,0,1:T(2,128)}), f32[2,1024,256]{2,0,1:T(2,128)}, u32[]{:S(2)}, u32[]{:S(2)}) %all-to-all-start.2) | async-done | bytes 2097184 | tf_op jit(solution)/shard_map/all_to_all | solution.py:51
  (133 shorter events, 64.2 us)
Async XLA Ops:
  7.2 2.5 copy-start.17
  7.2 3.1 copy-start.18
  9.7 1.7 copy-start.25
  17.2 5.8 %copy-start.21 = (bf16[2,1,64,512]{3,2,1,0:T(8,128)(2,1)S(1)}, bf16[2,1,64,512]{3,2,1,0:T(8,128)(2,1)}, u32[]{:S(2)}) copy-start(bf16[2,1,64,512]{3,2,1,0:T(8,128)(2,1)} %param.8) | copy-start | bytes 393220
  17.2 6.6 %copy-start.22 = (bf16[1,64,4,256]{3,2,1,0:T(4,128)(2,1)S(1)}, bf16[1,64,4,256]{3,2,1,0:T(4,128)(2,1)}, u32[]{:S(2)}) copy-start(bf16[1,64,4,256]{3,2,1,0:T(4,128)(2,1)} %param.7) | copy-start | bytes 393220
  17.2 43.1 %all-to-all-start = ((bf16[8,64,3072]{2,1,0:T(8,128)(2,1)}), bf16[8,64,3072]{2,1,0:T(8,128)(2,1)S(1)}, u32[]{:S(2)}, u32[]{:S(2)}) async-start(bf16[8,64,3072]{2,1,0:T(8,128)(2,1)} %copy.244), calls=%async_computation | async-start | bytes 6291456 | tf_op jit(solution)/shard_map/all_to_all | solution.py:84
  22.7 91.8 %all-gather.2.cloned.1.call-start = ((), (), s32[]{:S(2)}) async-start(), calls=%async_computation.5 | async-start | bytes 2228224 | tf_op jit(solution)/shard_map/all_gather | solution.py:67
  62.0 1.9 copy-start.13
  68.3 2.4 copy-start.23
  127.1 4.9 %copy-start.24 = (f32[9,4,2,64]{3,2,1,0:T(2,128)S(1)}, f32[9,4,2,64]{3,2,1,0:T(2,128)}, u32[]{:S(2)}) copy-start(f32[9,4,2,64]{3,2,1,0:T(2,128)} %get-tuple-element.51) | copy-start | bytes 55300
  132.0 7.0 %copy-start = (f32[4,9,64,2,1024]{4,2,3,1,0:T(8,128)}, f32[4,9,64,2,1024]{4,2,3,1,0:T(8,128)S(1)}, u32[]{:S(2)}) copy-start(f32[4,9,64,2,1024]{4,2,3,1,0:T(8,128)S(1)} %get-tuple-element.54) | copy-start | bytes 56623108
  132.0 1.5 copy-start.4
  146.1 1.4 copy-start.3
  146.1 1.4 copy-start.19
  157.3 3.1 copy-start.10
  179.2 1.5 copy-start.16
  183.5 5.2 %copy-start.6 = (bf16[9,64,4,2,128]{4,1,3,0,2:T(8,128)(2,1)S(1)}, bf16[9,64,4,2,128]{4,1,3,0,2:T(8,128)(2,1)}, u32[]{:S(2)}) copy-start(bf16[9,64,4,2,128]{4,1,3,0,2:T(8,128)(2,1)} %get-tuple-element.56) | copy-start | bytes 3538948
  190.9 2.8 slice-start.5
  195.4 8.6 %slice-start.1 = ((s8[9437184]{0:T(1024)(128)(4,1)}), s8[1048576]{0:T(1024)(128)(4,1)S(1)}, s32[]{:S(2)}) async-start(s8[9437184]{0:T(1024)(128)(4,1)} %bitcast.165), calls=%async_computation.7 | async-start | bytes 2097152
  198.1 5.9 %slice-start.2 = ((s8[9437184]{0:T(1024)(128)(4,1)}), s8[4194304]{0:T(1024)(128)(4,1)S(1)}, s32[]{:S(2)}) async-start(s8[9437184]{0:T(1024)(128)(4,1)} %bitcast.165), calls=%async_computation.8 | async-start | bytes 8388608
  198.1 6.5 %slice-start.3 = ((s8[9437184]{0:T(1024)(128)(4,1)}), s8[4194304]{0:T(1024)(128)(4,1)S(1)}, s32[]{:S(2)}) async-start(s8[9437184]{0:T(1024)(128)(4,1)} %bitcast.165), calls=%async_computation.9 | async-start | bytes 8388608
  198.1 6.7 %copy-start.14 = (bf16[1,1,1024,512]{2,3,1,0:T(8,128)(2,1)S(1)}, bf16[1,1,1024,512]{2,3,1,0:T(8,128)(2,1)}, u32[]{:S(2)}) copy-start(bf16[1,1,1024,512]{2,3,1,0:T(8,128)(2,1)} %copy.349) | copy-start | bytes 3145732
  207.5 3.6 copy-start.7
  223.8 12.0 %all-to-all-start.3 = ((f32[2,1,262144]{2,1,0:T(1,128)}), f32[2,1,262144]{2,1,0:T(1,128)S(1)}, u32[]{:S(2)}, u32[]{:S(2)}) async-start(f32[2,1,262144]{2,1,0:T(1,128)} %reshape.164), calls=%async_computation.3 | async-start | bytes 4194304 | tf_op jit(solution)/shard_map/all_to_all | solution.py:51
  235.7 1.4 copy-start.2
  237.1 26.3 %all-to-all-start.1 = ((f32[2,1024,512]{1,0,2:T(2,128)}), f32[2,1024,512]{1,0,2:T(2,128)}, u32[]{:S(2)}, u32[]{:S(2)}) async-start(f32[2,1024,512]{1,0,2:T(2,128)} %pad_maximum_fusion), calls=%async_computation.1 | async-start | bytes 8388608 | tf_op jit(solution)/shard_map/all_to_all | solution.py:51
  258.9 2.7 copy-start.11
  263.4 36.9 %all-to-all-start.4 = ((bf16[8,64,2560]{2,1,0:T(8,128)(2,1)}), bf16[8,64,2560]{2,1,0:T(8,128)(2,1)S(1)}, u32[]{:S(2)}, u32[]{:S(2)}) async-start(bf16[8,64,2560]{2,1,0:T(8,128)(2,1)} %pad_maximum_fusion.1), calls=%async_computation.4 | async-start | bytes 5242880 | tf_op jit(solution)/shard_map/all_to_all | solution.py:142
  279.9 28.9 %slice-start.4 = ((bf16[9,64,4,2,128]{4,1,3,0,2:T(8,128)(2,1)}), bf16[1,64,4,2,128]{4,1,3,0,2:T(8,128)(2,1)S(1)}, s32[]{:S(2)}) async-start(bf16[9,64,4,2,128]{4,1,3,0,2:T(8,128)(2,1)} %copy-done.7), calls=%async_computation.10 | async-start | bytes 262144 | tf_op jit(solution)/shard_map/slice | solution.py:154
  300.3 57.2 %all-to-all-start.2 = ((f32[2,1024,256]{2,0,1:T(2,128)}), f32[2,1024,256]{2,0,1:T(2,128)}, u32[]{:S(2)}, u32[]{:S(2)}) async-start(f32[2,1024,256]{2,0,1:T(2,128)} %copy.285), calls=%async_computation.2 | async-start | bytes 4194304 | tf_op jit(solution)/shard_map/all_to_all | solution.py:51
  311.6 1.5 copy-start.1
  313.1 2.8 slice-start
  (6 other events, 6.8 us)
Sparse Core Ops, SparseCore 0:
  26.7 87.7 all-gather.1

commit v4 on v3

--- a/solution.py
+++ b/solution.py
@@ -64,9 +64,11 @@
     peers = lax.axis_size("resp")
     kv_width = kv_heads * head_size
     q_width = kv_heads * local_width
-    gathered = lax.all_gather(prompt_kv, "prompt", axis=2, tiled=True)
-    prompt_keys = gathered[0, 0].reshape(full_len, kv_heads, head_size)
-    prompt_values = gathered[1, 0].reshape(full_len, kv_heads, head_size)
+    blocks = lax.axis_size("prompt")
+    repeated = jnp.broadcast_to(prompt_kv[:, 0][:, None], (2, blocks) + prompt_kv.shape[2:])
+    gathered = lax.all_to_all(repeated, "prompt", split_axis=1, concat_axis=1, tiled=True)
+    prompt_keys = gathered[0].reshape(full_len, kv_heads, head_size)
+    prompt_values = gathered[1].reshape(full_len, kv_heads, head_size)
 
     order = resp_prompt[0, 0]
     picker = (jnp.arange(peers)[:, None] == order[None, :]).astype(jnp.bfloat16)

time: 374 us -> 354 us (0.947)
  blocking collectives: 0 us -> 43.9 us
  waiting for transfers between devices: 136 us -> 94.9 us
  between operations: 15.1 us -> 1.68 us
  local copies, waits for them, and re-layouts: 97.8 us -> 85 us
    all_to_all x0 -> x1, blocking collectives: none -> 43.9 us  [body(): got = lax.all_to_all(send, 'resp', split_axis=0, concat_axis=0, tiled=True)]
    all_gather x1 -> x0, waiting for transfers between devices: 41.9 us -> none  [body(): gathered = lax.all_gather(prompt_kv, 'prompt', axis=2, tiled=True)]
    unnamed x75 -> x74, local copies, waits for them, and re-layouts: 38.4 us -> 26 us
    all_to_all x1, starting transfers between devices: 5.53 us -> 11.2 us  [body(): lax.all_to_all(repeated, 'prompt', split_axis=1, concat_axis=1, tiled=True)]
    another operation x0 -> x2, local copies, waits for them, and re-layouts: none -> 4.3 us  [the longest x1 2.17 us: body(): prompt_keys = gathered[0].reshape(full_len, kv_heads, head_size)]
  transfers between devices with their start and end apart: 6 -> 5, of which waited for: 4 -> 3; matrix products, arithmetic and copies ran while one was open for 18% -> 18% of each run, Pallas kernels for 0% -> 0%
where the time goes in v4:
time: 354 us; the launch traced here: 348 us
  waiting for transfers between devices  94.9 us (27%)
  local copies, waits for them, and re-layouts  85 us (24%)
  other arithmetic  46.7 us (13%)
  matrix products  45.9 us (13%)
  blocking collectives  43.9 us (12%)
  starting transfers between devices  29.8 us (8%)
    all_to_all x1, blocking collectives, body(): got = lax.all_to_all(send, 'resp', split_axis=0, concat_axis=0, tiled=True)  43.9 us
    all_to_all x3, waiting for transfers between devices, scatter_sum(): lax.all_to_all(x, axis_name, split_axis=dim, concat_axis=dim, tiled=True)  40.7 us
    all_to_all x1, waiting for transfers between devices, body(): lax.all_to_all(repeated, 'prompt', split_axis=1, concat_axis=1, tiled=True)  33.6 us
    unnamed x74, local copies, waits for them, and re-layouts  26 us
    all_to_all x1, waiting for transfers between devices, body(): ret = lax.all_to_all(back, 'resp', split_axis=0, concat_axis=0, tiled=True)  20.6 us
    all_to_all x3, starting transfers between devices, scatter_sum(): lax.all_to_all(x, axis_name, split_axis=dim, concat_axis=dim, tiled=True)  14.6 us
    dot_general x1, matrix products, attend_blocks(): jnp.einsum('brkgd,nkd->bkgrn', cotangent, values_in, preferred_element_ty...  13.9 us
    reduce_sum x3, other arithmetic, scatter_sum(): return jnp.sum(got.reshape(shape), axis=dim)  12.1 us
  transfers between devices with their start and end apart: 5, of which 3 were waited for; matrix products, arithmetic and copies ran while one was open for 18% of the time, Pallas kernels for 0%

profile of v4, /device:TPU:32, one launch (start us, length us, event | category | flops | bytes accessed | tf_op | source)
XLA Modules:
  0.0 347.8 jit_solution(4991744179448971192)
XLA Ops:
  0.7 2.5 copy.230
  9.0 43.9 %all_to_all.30 = bf16[8,64,3072]{2,1,0:T(8,128)(2,1)S(1)} all-to-all(bf16[8,64,3072]{2,1,0:T(8,128)(2,1)S(1)} %copy.234), channel_id=1, replica_groups=mesh['prompt'=16,'resp'=8,'head'=2] {'resp'}, dimensions={0} | all-to-all | bytes 6291456 | tf_op jit(solution)/shard_map/all_to_all | solution.py:86
  54.5 11.2 %all-to-all-start.1 = ((bf16[2,16,64,512]{3,2,0,1:T(8,128)(2,1)}), bf16[2,16,64,512]{3,2,0,1:T(8,128)(2,1)}, u32[]{:S(2)}, u32[]{:S(2)}) async-start(bf16[2,16,64,512]{3,2,0,1:T(8,128)(2,1)} %broadcast_in_dim.34), calls=%async_computation.1 | async-start | bytes 4194304 | tf_op jit(solution)/shard_map/all_to_all | solution.py:69
  72.6 2.6 concatenate.35
  80.7 33.6 %all-to-all-done.1 = bf16[2,16,64,512]{3,2,0,1:T(8,128)(2,1)} async-done(((bf16[2,16,64,512]{3,2,0,1:T(8,128)(2,1)}), bf16[2,16,64,512]{3,2,0,1:T(8,128)(2,1)}, u32[]{:S(2)}, u32[]{:S(2)}) %all-to-all-start.1) | async-done | bytes 2097184 | tf_op jit(solution)/shard_map/all_to_all | solution.py:69
  114.3 3.1 fusion.58
  119.6 5.2 %bitcast_reduce_fusion = (f32[9,4,2,64]{3,2,0,1:T(2,128)S(1)}, f32[4,9,64,2,1024]{4,2,3,1,0:T(8,128)S(1)}) fusion(pred[9,64,1024]{2,1,0:T(8,128)(4,1)} %concatenate.33, bf16[9,64,4,2,128]{4,1,3,0,2:T(8,128)(2,1)} %copy-done.8, bf16[1024,4,128,1,1]{2,1,0,4,3:T(4,128)(2,1)} %bitcast.170), kind=kOutput, calls=%fused_computation.5 | convolution fusion | flops 1222110720 | bytes 21710848 | tf_op jit(solution)/shard_map/brkgd,nkd->bkgrn/dot_general | solution.py:14
  126.2 5.4 %fusion.3 = f32[9,4,2,64]{3,2,0,1:T(2,128)S(1)} fusion(f32[4,9,64,2,1024]{4,2,3,1,0:T(8,128)S(1)} %get-tuple-element.54, f32[9,4,2,64]{3,2,0,1:T(2,128)S(1)} %copy.244, pred[9,64,1024]{2,1,0:T(8,128)(4,1)S(1)} %copy-done.4), kind=kLoop, calls=%fused_computation.7 | loop fusion | flops 18869760 | bytes 19501056 | tf_op jit(solution)/shard_map/reduce_sum | solution.py:21
  137.5 8.8 %fusion.5 = bf16[9,4,2,64,1024]{4,3,2,0,1:T(8,128)(2,1)S(1)} fusion(f32[4,9,64,2,1024]{4,2,3,1,0:T(8,128)} %copy-done, f32[9,4,2,64]{3,2,0,1:T(2,128)S(1)} %copy-done.20, pred[9,64,1024]{2,1,0:T(8,128)(4,1)S(1)} %copy-done.5), kind=kLoop, calls=%fused_computation.10 | loop fusion | flops 18874368 | bytes 28919808 | tf_op jit(solution)/shard_map/convert_element_type | solution.py:27
  146.3 3.1 fusion.6
  149.4 3.8 %fusion.20 = (f32[9,4,2,64]{3,2,0,1:T(2,128)S(1)}, bf16[9,64,4,2,128]{4,1,3,0,2:T(8,128)(2,1)}) fusion(bf16[9,64,4,2,128]{4,1,3,0,2:T(8,128)(2,1)S(1)} %copy_dynamic-update-slice_fusion.2, f32[9,4,128,2,64]{2,4,3,0,1:T(8,128)S(1)} %fusion.29, bf16[9,4,2,64,1024]{4,3,2,0,1:T(8,128)(2,1)S(1)} %fusion.5, bf16[1024,4,128,1,1]{2,1,0,4,3:T(4,128)(2,1)S(1)} %bitcast.164), kind=kOutput, calls=%fused_computation.32 | convolution fusion | flops 1211493888 | bytes 15222784 | tf_op jit(solution)/shard_map/bkgrn,nkd->brkgd/dot_general | solution.py:30
  153.1 13.9 %fusion.1 = bf16[9,4,2,64,1024]{4,3,2,0,1:T(8,128)(2,1)} fusion(f32[4,9,64,2,1024]{4,2,3,1,0:T(8,128)} %copy-done, f32[9,4,2,64]{3,2,0,1:T(2,128)S(1)} %get-tuple-element.55, f32[9,4,2,64]{3,2,0,1:T(2,128)S(1)} %copy-done.20, pred[9,64,1024]{2,1,0:T(8,128)(4,1)S(1)} %copy-done.5, bf16[9,64,4,2,128]{4,1,3,0,2:T(8,128)(2,1)S(1)} %copy_dynamic-update-slice_fusion.2, ...), kind=kOutput, calls=%fused_computation.2 | convolution fusion | flops 1236271104 | bytes 31166464 | tf_op jit(solution)/shard_map/brkgd,nkd->bkgrn/dot_general | solution.py:34
  172.6 5.2 %copy.270 = f32[1,1024,512]{1,0,2:T(1,128)} copy(f32[1,1024,512]{1,2,0:T(8,128)} %bitcast.174) | data formatting | bytes 4194304 | tf_op jit(solution)/shard_map/stack | solution.py:127
  179.9 2.8 reshape.138
  184.5 2.7 stack.21
  187.2 5.8 %bitcast_multiply_fusion = f32[4,128,1024]{2,1,0:T(8,128)S(1)} fusion(bf16[9,4,2,64,1024]{4,3,2,0,1:T(8,128)(2,1)} %fusion.1, bf16[9,64,4,2,128]{4,1,3,0,2:T(8,128)(2,1)} %copy-done.8), kind=kOutput, calls=%fused_computation.39 | convolution fusion | flops 1208483840 | bytes 12713984 | tf_op jit(solution)/shard_map/bkgrn,brkgd->nkd/dot_general | solution.py:42
  193.9 2.6 fusion.17
  196.6 3.6 %copy.269 = f32[1,1024,512]{1,0,2:T(1,128)} copy(f32[1,1024,512]{1,2,0:T(8,128)S(1)} %bitcast.175) | data formatting | bytes 4194304 | tf_op jit(solution)/shard_map/stack | solution.py:127
  203.9 3.8 %copy.279 = f32[8,2,64,512]{2,0,1,3:T(8,128)} copy(f32[8,2,64,512]{3,2,0,1:T(8,128)S(1)} %pad_maximum_fusion.2) | data formatting | bytes 4194304 | tf_op jit(solution)/shard_map/stack | solution.py:130
  207.6 5.2 %reshape.164 = f32[2,1,262144]{2,1,0:T(1,128)} reshape(f32[512,2,8,64]{3,2,1,0:T(8,128)} %bitcast.159) | data formatting | bytes 4194304
  212.8 4.0 %all-to-all-start.4 = ((f32[2,1,262144]{2,1,0:T(1,128)}), f32[2,1,262144]{2,1,0:T(1,128)S(1)}, u32[]{:S(2)}, u32[]{:S(2)}) async-start(f32[2,1,262144]{2,1,0:T(1,128)} %reshape.164), calls=%async_computation.4 | async-start | bytes 4194304 | tf_op jit(solution)/shard_map/all_to_all | solution.py:51
  216.8 8.0 %pad_maximum_fusion = f32[2,1024,512]{1,0,2:T(2,128)} fusion(f32[1,1024,512]{1,0,2:T(1,128)} %copy.270, f32[1,1024,512]{1,0,2:T(1,128)} %copy.269), kind=kLoop, calls=%fused_computation.17 | loop fusion | flops 1048576 | bytes 8388608 | tf_op jit(solution)/shard_map/stack | solution.py:127
  226.2 5.6 %all-to-all-start.2 = ((f32[2,1024,512]{1,0,2:T(2,128)}), f32[2,1024,512]{1,0,2:T(2,128)}, u32[]{:S(2)}, u32[]{:S(2)}) async-start(f32[2,1024,512]{1,0,2:T(2,128)} %pad_maximum_fusion), calls=%async_computation.2 | async-start | bytes 8388608 | tf_op jit(solution)/shard_map/all_to_all | solution.py:51
  232.3 8.1 %reduce.2 = f32[2,262144]{1,0:T(2,128)S(1)} reduce(f32[2,1,262144]{2,1,0:T(1,128)} %copy-done.2, f32[]{:T(128)} %broadcast.42), dimensions={1}, to_apply=%all_to_all.22.reduce_sub_computation | reduce | bytes 4194308 | tf_op jit(solution)/shard_map/all_to_all | solution.py:51
  240.4 4.3 %reshape.165 = f32[512,2,8,64]{3,2,1,0:T(8,128)} reshape(f32[2,262144]{1,0:T(2,128)S(1)} %reduce.2) | data formatting | bytes 4194304
  244.7 3.3 reduce_sum.49
  252.5 3.9 %all-to-all-start.5 = ((bf16[8,64,2560]{2,1,0:T(8,128)(2,1)}), bf16[8,64,2560]{2,1,0:T(8,128)(2,1)S(1)}, u32[]{:S(2)}, u32[]{:S(2)}) async-start(bf16[8,64,2560]{2,1,0:T(8,128)(2,1)} %pad_maximum_fusion.1), calls=%async_computation.5 | async-start | bytes 5242880 | tf_op jit(solution)/shard_map/all_to_all | solution.py:144
  256.3 6.6 %reduce_sum.47 = f32[2,1024,256]{1,0,2:T(2,128)} reduce(f32[2,1024,2,256]{1,0,3,2:T(2,128)} %bitcast.39, f32[]{:T(128)} %constant.8.clone.1), dimensions={2}, to_apply=%region_4.5 | reduce | flops 524288 | bytes 6291460 | tf_op jit(solution)/shard_map/reduce_sum | solution.py:53
  263.0 5.3 %copy.272 = f32[2,1024,256]{2,0,1:T(2,128)} copy(f32[2,1024,256]{1,0,2:T(2,128)} %reduce_sum.47) | data formatting | bytes 4194304 | tf_op jit(solution)/shard_map/reduce_sum | solution.py:53
  268.3 20.6 %all-to-all-done.5 = bf16[8,64,2560]{2,1,0:T(8,128)(2,1)S(1)} async-done(((bf16[8,64,2560]{2,1,0:T(8,128)(2,1)}), bf16[8,64,2560]{2,1,0:T(8,128)(2,1)S(1)}, u32[]{:S(2)}, u32[]{:S(2)}) %all-to-all-start.5) | async-done | bytes 2621472 | tf_op jit(solution)/shard_map/all_to_all | solution.py:144
  288.9 5.0 %all-to-all-start.3 = ((f32[2,1024,256]{2,0,1:T(2,128)}), f32[2,1024,256]{2,0,1:T(2,128)}, u32[]{:S(2)}, u32[]{:S(2)}) async-start(f32[2,1024,256]{2,0,1:T(2,128)} %copy.272), calls=%async_computation.3 | async-start | bytes 4194304 | tf_op jit(solution)/shard_map/all_to_all | solution.py:51
  303.7 40.7 %all-to-all-done.3 = f32[2,1024,256]{2,0,1:T(2,128)} async-done(((f32[2,1024,256]{2,0,1:T(2,128)}), f32[2,1024,256]{2,0,1:T(2,128)}, u32[]{:S(2)}, u32[]{:S(2)}) %all-to-all-start.3) | async-done | bytes 2097184 | tf_op jit(solution)/shard_map/all_to_all | solution.py:51
  (133 shorter events, 62.0 us)
Async XLA Ops:
  0.6 2.5 copy-start.17
  0.6 3.1 copy-start.18
  3.1 1.7 copy-start.26
  9.0 43.9 %copy-start.21 = (bf16[2,1,64,512]{3,2,1,0:T(8,128)(2,1)S(1)}, bf16[2,1,64,512]{3,2,1,0:T(8,128)(2,1)}, u32[]{:S(2)}) copy-start(bf16[2,1,64,512]{3,2,1,0:T(8,128)(2,1)} %param.8) | copy-start | bytes 393220
  54.5 11.3 %copy-start.22 = (bf16[1,64,4,256]{3,2,1,0:T(4,128)(2,1)S(1)}, bf16[1,64,4,256]{3,2,1,0:T(4,128)(2,1)}, u32[]{:S(2)}) copy-start(bf16[1,64,4,256]{3,2,1,0:T(4,128)(2,1)} %param.7) | copy-start | bytes 393220
  54.5 11.3 %copy-start.23 = (bf16[1,64,4,256]{3,2,1,0:T(4,128)(2,1)S(1)}, bf16[1,64,4,256]{3,2,1,0:T(4,128)(2,1)}, u32[]{:S(2)}) copy-start(bf16[1,64,4,256]{3,2,1,0:T(4,128)(2,1)} %param.9) | copy-start | bytes 393220
  54.5 59.8 %all-to-all-start.1 = ((bf16[2,16,64,512]{3,2,0,1:T(8,128)(2,1)}), bf16[2,16,64,512]{3,2,0,1:T(8,128)(2,1)}, u32[]{:S(2)}, u32[]{:S(2)}) async-start(bf16[2,16,64,512]{3,2,0,1:T(8,128)(2,1)} %broadcast_in_dim.34), calls=%async_computation.1 | async-start | bytes 4194304 | tf_op jit(solution)/shard_map/all_to_all | solution.py:69
  70.1 1.9 copy-start.13
  76.4 2.4 copy-start.24
  119.6 5.2 %copy-start.25 = (f32[9,4,2,64]{3,2,1,0:T(2,128)S(1)}, f32[9,4,2,64]{3,2,1,0:T(2,128)}, u32[]{:S(2)}) copy-start(f32[9,4,2,64]{3,2,1,0:T(2,128)} %get-tuple-element.51) | copy-start | bytes 55300
  124.7 6.9 %copy-start = (f32[4,9,64,2,1024]{4,2,3,1,0:T(8,128)}, f32[4,9,64,2,1024]{4,2,3,1,0:T(8,128)S(1)}, u32[]{:S(2)}) copy-start(f32[4,9,64,2,1024]{4,2,3,1,0:T(8,128)S(1)} %get-tuple-element.54) | copy-start | bytes 56623108
  124.7 1.5 copy-start.4
  135.0 1.4 copy-start.3
  135.1 1.4 copy-start.19
  146.3 3.1 copy-start.11
  168.3 1.5 copy-start.16
  172.6 5.2 %copy-start.6 = (bf16[9,64,4,2,128]{4,1,3,0,2:T(8,128)(2,1)S(1)}, bf16[9,64,4,2,128]{4,1,3,0,2:T(8,128)(2,1)}, u32[]{:S(2)}) copy-start(bf16[9,64,4,2,128]{4,1,3,0,2:T(8,128)(2,1)} %get-tuple-element.56) | copy-start | bytes 3538948
  179.9 2.9 slice-start.5
  184.4 8.6 %slice-start.1 = ((s8[9437184]{0:T(1024)(128)(4,1)}), s8[1048576]{0:T(1024)(128)(4,1)S(1)}, s32[]{:S(2)}) async-start(s8[9437184]{0:T(1024)(128)(4,1)} %bitcast.162), calls=%async_computation.7 | async-start | bytes 2097152
  187.2 5.9 %slice-start.2 = ((s8[9437184]{0:T(1024)(128)(4,1)}), s8[4194304]{0:T(1024)(128)(4,1)S(1)}, s32[]{:S(2)}) async-start(s8[9437184]{0:T(1024)(128)(4,1)} %bitcast.162), calls=%async_computation.8 | async-start | bytes 8388608
  187.2 6.5 %slice-start.3 = ((s8[9437184]{0:T(1024)(128)(4,1)}), s8[4194304]{0:T(1024)(128)(4,1)S(1)}, s32[]{:S(2)}) async-start(s8[9437184]{0:T(1024)(128)(4,1)} %bitcast.162), calls=%async_computation.9 | async-start | bytes 8388608
  187.2 6.7 %copy-start.14 = (bf16[1024,4,128]{2,1,0:T(4,128)(2,1)S(1)}, bf16[1024,4,128]{2,1,0:T(4,128)(2,1)}, u32[]{:S(2)}) copy-start(bf16[1024,4,128]{2,1,0:T(4,128)(2,1)} %reshape_squeeze.16) | copy-start | bytes 3145732
  196.6 3.6 %copy-start.7 = (bf16[9,64,4,2,128]{4,1,3,0,2:T(8,128)(2,1)}, bf16[9,64,4,2,128]{4,1,3,0,2:T(8,128)(2,1)S(1)}, u32[]{:S(2)}) copy-start(bf16[9,64,4,2,128]{4,1,3,0,2:T(8,128)(2,1)S(1)} %fusion.17) | copy-start | bytes 3538948
  212.8 11.9 %all-to-all-start.4 = ((f32[2,1,262144]{2,1,0:T(1,128)}), f32[2,1,262144]{2,1,0:T(1,128)S(1)}, u32[]{:S(2)}, u32[]{:S(2)}) async-start(f32[2,1,262144]{2,1,0:T(1,128)} %reshape.164), calls=%async_computation.4 | async-start | bytes 4194304 | tf_op jit(solution)/shard_map/all_to_all | solution.py:51
  224.8 1.4 copy-start.2
  226.2 26.3 %all-to-all-start.2 = ((f32[2,1024,512]{1,0,2:T(2,128)}), f32[2,1024,512]{1,0,2:T(2,128)}, u32[]{:S(2)}, u32[]{:S(2)}) async-start(f32[2,1024,512]{1,0,2:T(2,128)} %pad_maximum_fusion), calls=%async_computation.2 | async-start | bytes 8388608 | tf_op jit(solution)/shard_map/all_to_all | solution.py:51
  248.0 2.7 copy-start.10
  252.5 36.4 %all-to-all-start.5 = ((bf16[8,64,2560]{2,1,0:T(8,128)(2,1)}), bf16[8,64,2560]{2,1,0:T(8,128)(2,1)S(1)}, u32[]{:S(2)}, u32[]{:S(2)}) async-start(bf16[8,64,2560]{2,1,0:T(8,128)(2,1)} %pad_maximum_fusion.1), calls=%async_computation.5 | async-start | bytes 5242880 | tf_op jit(solution)/shard_map/all_to_all | solution.py:144
  268.3 27.5 %slice-start.4 = ((bf16[9,64,4,2,128]{4,1,3,0,2:T(8,128)(2,1)}), bf16[1,64,4,2,128]{4,1,3,0,2:T(8,128)(2,1)S(1)}, s32[]{:S(2)}) async-start(bf16[9,64,4,2,128]{4,1,3,0,2:T(8,128)(2,1)} %copy-done.7), calls=%async_computation.10 | async-start | bytes 262144 | tf_op jit(solution)/shard_map/slice | solution.py:156
  288.9 55.5 %all-to-all-start.3 = ((f32[2,1024,256]{2,0,1:T(2,128)}), f32[2,1024,256]{2,0,1:T(2,128)}, u32[]{:S(2)}, u32[]{:S(2)}) async-start(f32[2,1024,256]{2,0,1:T(2,128)} %copy.272), calls=%async_computation.3 | async-start | bytes 4194304 | tf_op jit(solution)/shard_map/all_to_all | solution.py:51
  298.5 1.5 copy-start.1
  300.0 2.8 slice-start
  (6 other events, 6.8 us)
